TPU v7x, 32 devices: a whole 2x2x4 slice. The times are simulated.
32 devices in a mesh: grad: 4 (over y, x), col: 8 (over z, core).
Axes of the slice: x: 2, y: 2, z: 4, core: 2. Of those that a mesh axis runs over, the one named last changes fastest.
Arguments:
- gradient: bfloat16 [16384, 53248], P(('grad', 'col'))
- test_matrix: bfloat16 [16384, 256], P(('grad', 'col')), may hold values from -6 to 6
Outputs:
- low_rank: float32 [16384, 256], P(('grad', 'col'))
- projector: float32 [53248, 256], P('col')
All inputs are finite; a program needn't handle non-finite values.
Results may differ from a plain program's by a relative error of at most 0.008.
Values may be sent and summed in bfloat16 or wider, within the bound.
No kernel may reach another device: no remote copies, remote signals or barrier semaphores. Data moves between devices by JAX's collectives and lax.ppermute only.
A program may use at most 256 MiB of HBM per device.

v0:
```python
import math

import jax
import jax.numpy as jnp
from jax import lax
from jax.sharding import PartitionSpec as P

FF = 53248
POWER = 2


def orthonormal(matrix, reduce_gram):
    partial_gram = lax.dot_general(
        matrix,
        matrix,
        (((0,), (0,)), ((), ())),
        precision=lax.Precision.HIGHEST,
        preferred_element_type=jnp.float32,
    )
    gram = reduce_gram(partial_gram)
    lower_factor = jnp.linalg.cholesky(gram)
    return lax.linalg.triangular_solve(
        lower_factor, matrix, left_side=False, lower=True, transpose_a=True
    )


def gram_over_columns(partial_gram):
    return lax.psum(partial_gram, "col")


def shards(gradient, test_matrix):
    blocks = lax.all_to_all(gradient, "col", split_axis=1, concat_axis=0, tiled=True)

    def add_sketch(row_piece):
        return lax.dot_general(
            blocks, row_piece, (((0,), (0,)), ((), ())), preferred_element_type=jnp.float32
        )

    sketch = add_sketch(lax.all_gather(test_matrix, "col", axis=0, tiled=True))
    for iteration in range(POWER + 1):
        summed = lax.psum(sketch, "grad")
        basis_block = orthonormal(summed, gram_over_columns)
        basis_bf = basis_block.astype(jnp.bfloat16)
        reduced = lax.psum_scatter(
            jnp.dot(blocks, basis_bf, preferred_element_type=jnp.float32),
            "col",
            scatter_dimension=0,
            tiled=True,
        )
        if iteration < POWER:
            reduced_bf = reduced.astype(jnp.bfloat16)
            sketch = add_sketch(lax.all_gather(reduced_bf, "col", axis=0, tiled=True))
    return (reduced, basis_block * math.sqrt(FF))


def solution(mesh):
    return jax.shard_map(
        shards,
        mesh=mesh,
        in_specs=(P(("grad", "col"), None), P(("grad", "col"), None)),
        out_specs=(P(("grad", "col"), None), P("col", None)),
        check_vma=False,
    )
```

profile of v0, /device:TPU:0, one launch (start us, length us, event | category | flops | bytes accessed | tf_op | source)
XLA Modules:
  0.0 2603.3 jit_solution(11232503956803364355)
XLA Ops:
  7.2 70.6 %copy.20 = bf16[512,53248]{0,1:T(8,128)(2,1)} copy(bf16[512,53248]{1,0:T(8,128)(2,1)} %param.5) | data formatting | bytes 109051904 | tf_op args[0]
  77.8 8.8 all-to-all-start
  87.4 1189.5 %all-to-all-done = bf16[512,8,6656]{0,2,1:T(8,128)(2,1)} async-done(((bf16[512,8,6656]{0,2,1:T(8,128)(2,1)}), bf16[512,8,6656]{0,2,1:T(8,128)(2,1)}, u32[]{:S(2)}, u32[]{:S(2)}) %all-to-all-start) | async-done | bytes 54525984 | tf_op jit(solution)/shard_map/all_to_all | solution.py:32
  1276.9 64.6 %copy.21 = bf16[8,512,6656]{2,1,0:T(8,128)(2,1)} copy(bf16[8,512,6656]{1,2,0:T(8,128)(2,1)} %bitcast.1) | data formatting | bytes 109051904 | tf_op jit(solution)/shard_map/all_to_all | solution.py:32
  1341.5 25.8 fusion.41
  1367.9 145.9 %all-reduce.8.cloned.1.call-done = f32[6656,256]{1,0:T(8,128)} async-done(((f32[6656,256]{1,0:T(8,128)}), f32[6656,256]{1,0:T(8,128)}) %all-reduce.8.cloned.1.call-update) | async-done | bytes 6815760 | tf_op jit(solution)/shard_map/psum | solution.py:41
  1513.8 16.6 fusion.42
  1530.7 55.3 %all-reduce.10.cloned.1.call-done = f32[256,256]{0,1:T(8,128)} async-done(((f32[256,256]{0,1:T(8,128)}), f32[256,256]{0,1:T(8,128)}) %all-reduce.10.cloned.1.call-update) | async-done | bytes 262160 | tf_op jit(solution)/shard_map/psum | solution.py:28
  1586.0 1.1 copy.23
  1587.1 1.0 fusion.11
  1588.1 11.7 cholesky.172
  1599.8 9.8 custom-call.15
  1610.2 11.7 cholesky.189
  1624.0 4.2 while.6
  1624.8 1.4 bitcast_dynamic-update-slice_fusion.6
  1626.8 1.4 bitcast_dynamic-update-slice_fusion.6
  1628.9 19.7 custom-call.16
  1648.6 5.2 fusion.7
  1653.8 6.5 convolution_subtract_fusion.2
  1660.3 4.6 fusion.20
  1665.0 24.3 convolution_bitcast_fusion.4
  1689.4 49.1 %reduce-scatter.4.cloned.1.call-done = f32[512,256]{0,1:T(8,128)} async-done(((f32[4096,256]{0,1:T(8,128)}), f32[512,256]{0,1:T(8,128)}) %reduce-scatter.4.cloned.1.call-update) | async-done | bytes 524304 | tf_op jit(solution)/shard_map/reduce_scatter | solution.py:44
  1738.4 1.8 convert_element_type.16
  1740.3 27.8 %all-gather.6.cloned.1.call-done = bf16[4096,256]{0,1:T(8,128)(2,1)} async-done(((bf16[512,256]{0,1:T(8,128)(2,1)}), bf16[4096,256]{0,1:T(8,128)(2,1)}) %all-gather.6.cloned.1.call-update) | async-done | bytes 2097168 | tf_op jit(solution)/shard_map/all_gather | solution.py:52
  1768.1 25.5 convolution_bitcast_fusion.1
  1793.7 146.3 %all-reduce.12.cloned.1.call-done = f32[6656,256]{0,1:T(8,128)} async-done(((f32[6656,256]{0,1:T(8,128)}), f32[6656,256]{0,1:T(8,128)}) %all-reduce.12.cloned.1.call-update) | async-done | bytes 6815760 | tf_op jit(solution)/shard_map/psum | solution.py:41
  1940.0 19.3 fusion.43
  1959.5 55.4 %all-reduce.14.cloned.1.call-done = f32[256,256]{0,1:T(8,128)} async-done(((f32[256,256]{0,1:T(8,128)}), f32[256,256]{0,1:T(8,128)}) %all-reduce.14.cloned.1.call-update) | async-done | bytes 262160 | tf_op jit(solution)/shard_map/psum | solution.py:28
  2014.9 1.1 copy.25
  2016.0 1.0 fusion.10
  2017.0 11.7 cholesky.206
  2028.8 9.8 custom-call.17
  2039.1 11.7 cholesky.223
  2053.4 4.2 while.7
  2054.3 1.4 bitcast_dynamic-update-slice_fusion.7
  2056.3 1.4 bitcast_dynamic-update-slice_fusion.7
  2058.4 19.7 custom-call.18
  2078.0 5.2 fusion.5
  2083.2 4.2 convolution_subtract_fusion.1
  2087.4 4.3 fusion.16
  2091.7 24.7 convolution_bitcast_fusion.3
  2116.4 49.1 %reduce-scatter.6.cloned.1.call-done = f32[512,256]{0,1:T(8,128)} async-done(((f32[4096,256]{0,1:T(8,128)}), f32[512,256]{0,1:T(8,128)}) %reduce-scatter.6.cloned.1.call-update) | async-done | bytes 524304 | tf_op jit(solution)/shard_map/reduce_scatter | solution.py:44
  2165.5 1.8 convert_element_type.18
  2167.4 28.0 %all-gather.8.cloned.1.call-done = bf16[4096,256]{0,1:T(8,128)(2,1)} async-done(((bf16[512,256]{0,1:T(8,128)(2,1)}), bf16[4096,256]{0,1:T(8,128)(2,1)}) %all-gather.8.cloned.1.call-update) | async-done | bytes 2097168 | tf_op jit(solution)/shard_map/all_gather | solution.py:52
  2195.4 25.5 convolution_bitcast_fusion
  2221.0 146.3 %all-reduce.16.cloned.1.call-done = f32[6656,256]{0,1:T(8,128)} async-done(((f32[6656,256]{0,1:T(8,128)}), f32[6656,256]{0,1:T(8,128)}) %all-reduce.16.cloned.1.call-update) | async-done | bytes 6815760 | tf_op jit(solution)/shard_map/psum | solution.py:41
  2367.2 19.3 fusion.44
  2386.8 55.4 %all-reduce.18.cloned.1.call-done = f32[256,256]{0,1:T(8,128)} async-done(((f32[256,256]{0,1:T(8,128)}), f32[256,256]{0,1:T(8,128)}) %all-reduce.18.cloned.1.call-update) | async-done | bytes 262160 | tf_op jit(solution)/shard_map/psum | solution.py:28
  2442.2 1.1 copy.28
  2444.2 11.7 cholesky.240
  2456.0 9.8 custom-call.19
  2466.3 11.7 cholesky.257
  2480.7 4.2 while.8
  2481.5 1.4 bitcast_dynamic-update-slice_fusion.8
  2483.5 1.4 bitcast_dynamic-update-slice_fusion.8
  2485.6 19.7 custom-call.20
  2505.3 5.2 fusion.3
  2510.5 4.2 convolution_subtract_fusion
  2514.7 4.9 fusion.12
  2519.6 25.4 convolution_bitcast_fusion.2
  2545.0 5.4 fusion
  2550.4 8.1 copy.31
  2558.5 35.7 %reduce-scatter.8.cloned.1.call-done = f32[512,256]{0,1:T(8,128)} async-done(((f32[4096,256]{0,1:T(8,128)}), f32[512,256]{0,1:T(8,128)}) %reduce-scatter.8.cloned.1.call-update) | async-done | bytes 524304 | tf_op jit(solution)/shard_map/reduce_scatter | solution.py:44
  2594.2 2.0 copy.30
  (81 shorter events, 14.2 us)
Async XLA Ops:
  77.8 1199.1 %all-to-all-start = ((bf16[512,8,6656]{0,2,1:T(8,128)(2,1)}), bf16[512,8,6656]{0,2,1:T(8,128)(2,1)}, u32[]{:S(2)}, u32[]{:S(2)}) async-start(bf16[512,8,6656]{0,2,1:T(8,128)(2,1)} %bitcast.124), calls=%async_computation | async-start | bytes 109051904 | tf_op jit(solution)/shard_map/all_to_all | solution.py:32
  86.6 1254.9 %all-gather.4.cloned.1.call-start = ((), (), s32[]{:S(2)}) async-start(), calls=%async_computation.4 | async-start | bytes 2359296 | tf_op jit(solution)/shard_map/all_gather | solution.py:39
  87.3 1426.5 %all-reduce.8.cloned.1.call-start = ((), (), s32[]{:S(2)}) async-start(), calls=%async_computation.5 | async-start | bytes 13631488 | tf_op jit(solution)/shard_map/psum | solution.py:41
  1367.4 218.6 %all-reduce.10.cloned.1.call-start = ((), (), s32[]{:S(2)}) async-start(), calls=%async_computation.6 | async-start | bytes 524288 | tf_op jit(solution)/shard_map/psum | solution.py:28
  1530.4 208.0 %reduce-scatter.4.cloned.1.call-start = ((), (), s32[]{:S(2)}) async-start(), calls=%async_computation.7 | async-start | bytes 4718592 | tf_op jit(solution)/shard_map/reduce_scatter | solution.py:44
  1628.2 0.7 copy-start.4
  1648.6 5.2 copy-start
  1689.3 78.8 %all-gather.6.cloned.1.call-start = ((), (), s32[]{:S(2)}) async-start(), calls=%async_computation.8 | async-start | bytes 2359296 | tf_op jit(solution)/shard_map/all_gather | solution.py:52
  1740.2 199.7 %all-reduce.12.cloned.1.call-start = ((), (), s32[]{:S(2)}) async-start(), calls=%async_computation.9 | async-start | bytes 13631488 | tf_op jit(solution)/shard_map/psum | solution.py:41
  1793.7 221.2 %all-reduce.14.cloned.1.call-start = ((), (), s32[]{:S(2)}) async-start(), calls=%async_computation.10 | async-start | bytes 524288 | tf_op jit(solution)/shard_map/psum | solution.py:28
  1959.3 206.2 %reduce-scatter.6.cloned.1.call-start = ((), (), s32[]{:S(2)}) async-start(), calls=%async_computation.11 | async-start | bytes 4718592 | tf_op jit(solution)/shard_map/reduce_scatter | solution.py:44
  2057.6 0.7 copy-start.5
  2078.0 5.2 copy-start.2
  2116.4 79.0 %all-gather.8.cloned.1.call-start = ((), (), s32[]{:S(2)}) async-start(), calls=%async_computation.12 | async-start | bytes 2359296 | tf_op jit(solution)/shard_map/all_gather | solution.py:52
  2167.3 199.9 %all-reduce.16.cloned.1.call-start = ((), (), s32[]{:S(2)}) async-start(), calls=%async_computation.13 | async-start | bytes 13631488 | tf_op jit(solution)/shard_map/psum | solution.py:41
  2220.9 221.2 %all-reduce.18.cloned.1.call-start = ((), (), s32[]{:S(2)}) async-start(), calls=%async_computation.14 | async-start | bytes 524288 | tf_op jit(solution)/shard_map/psum | solution.py:28
  2386.6 207.6 %reduce-scatter.8.cloned.1.call-start = ((), (), s32[]{:S(2)}) async-start(), calls=%async_computation.15 | async-start | bytes 4718592 | tf_op jit(solution)/shard_map/reduce_scatter | solution.py:44
  2484.9 0.7 copy-start.3
  2505.3 5.2 copy-start.1
Sparse Core Ops, SparseCore 0:
  89.0 49.5 all-gather.3
  1367.5 146.2 all-reduce.7
  1530.6 55.4 all-reduce.9
  1689.4 48.9 reduce-scatter.3
  1740.5 27.5 all-gather.5
  1793.8 146.1 all-reduce.11
  1959.4 55.4 all-reduce.13
  2116.5 48.9 reduce-scatter.5
  2167.7 27.5 all-gather.7
  2221.0 146.1 all-reduce.15
  2386.7 55.4 all-reduce.17
  2545.2 48.9 reduce-scatter.7
where the time goes:
time: 2610 us; the launch traced here: 2600 us
  waiting for transfers between devices  1980 us (76%)
  matrix products  252 us (10%)
  other arithmetic  174 us (7%)
  local copies, waits for them, and re-layouts  163 us (6%)
    all_to_all x1, waiting for transfers between devices, shards(): lax.all_to_all(gradient, 'col', split_axis=1, concat_axis=0, tiled=True)  1190 us
    psum x3, waiting for transfers between devices, shards(): summed = lax.psum(sketch, 'grad')  438 us
    psum x3, waiting for transfers between devices, gram_over_columns(): return lax.psum(partial_gram, 'col')  166 us
    reduce_scatter x3, waiting for transfers between devices, shards(): lax.psum_scatter(jnp.dot(blocks, basis_bf, preferred_element_type=jnp.flo...  134 us
    another operation x20, other arithmetic, orthonormal(): lower_factor = jnp.linalg.cholesky(gram)  103 us
    unnamed x15, local copies, waits for them, and re-layouts  82.9 us
    dot_general x3, matrix products, add_sketch(): lax.dot_general(blocks, row_piece, (((0,), (0,)), ((), ())), preferred_el...  76.9 us
    dot_general x3, matrix products, shards(): jnp.dot(blocks, basis_bf, preferred_element_type=jnp.float32)  74.4 us
  transfers between devices with their start and end apart: 13, of which 12 were waited for; matrix products, arithmetic and copies ran while one was open for 3% of the time, Pallas kernels for 0%

commit v1 on v0

v1 whole, which is shorter than its diff:
```python
import math

import jax
import jax.numpy as jnp
from jax import lax
from jax.sharding import PartitionSpec as P

FF = 53248
POWER = 2


def orthonormal(rows):
    partial_gram = lax.dot_general(
        rows,
        rows,
        (((0,), (0,)), ((), ())),
        precision=lax.Precision.HIGHEST,
        preferred_element_type=jnp.float32,
    )
    gram = lax.psum(partial_gram, ("grad", "col"))
    lower_factor = jnp.linalg.cholesky(gram)
    return lax.linalg.triangular_solve(
        lower_factor, rows, left_side=False, lower=True, transpose_a=True
    )


def shards(gradient, test_matrix):
    n_grad = lax.axis_size("grad")
    n_col = lax.axis_size("col")
    n_rows, n_ff = gradient.shape
    piece = n_ff // (n_col * n_grad)
    split = gradient.reshape(n_rows, n_col, n_grad, piece)
    blocks = lax.all_to_all(split, "grad", split_axis=2, concat_axis=0, tiled=True)
    blocks = blocks.reshape(n_grad * n_rows, n_col * piece)

    def sketch_of(row_piece):
        rows = lax.all_gather(row_piece, "grad", axis=0, tiled=True)
        partial = lax.dot_general(
            blocks, rows, (((0,), (0,)), ((), ())), preferred_element_type=jnp.float32
        )
        return lax.psum_scatter(partial, "col", scatter_dimension=0, tiled=True)

    sketch = sketch_of(test_matrix)
    for iteration in range(POWER + 1):
        basis_rows = orthonormal(sketch)
        basis_bf = lax.all_gather(basis_rows.astype(jnp.bfloat16), "col", axis=0, tiled=True)
        reduced = lax.psum_scatter(
            jnp.dot(blocks, basis_bf, preferred_element_type=jnp.float32),
            "grad",
            scatter_dimension=0,
            tiled=True,
        )
        if iteration < POWER:
            sketch = sketch_of(reduced.astype(jnp.bfloat16))
    projector = lax.all_gather(basis_rows * math.sqrt(FF), "grad", axis=0, tiled=True)
    return (reduced, projector)


def solution(mesh):
    return jax.shard_map(
        shards,
        mesh=mesh,
        in_specs=(P(("grad", "col"), None), P(("grad", "col"), None)),
        out_specs=(P(("grad", "col"), None), P("col", None)),
        check_vma=False,
    )
```

time: 2610 us -> 2370 us (0.908)
  waiting for transfers between devices: 1980 us -> 1800 us
  matrix products: 252 us -> 184 us
    all_to_all x1, waiting for transfers between devices: 1190 us -> 596 us  [shards(): lax.all_to_all(split, 'grad', split_axis=2, concat_axis=0, tiled=True)]
    reduce_scatter x0 -> x3, waiting for transfers between devices: none -> 417 us  [sketch_of(): return lax.psum_scatter(partial, 'col', scatter_dimension=0, tiled=True)]
    all_gather x3 -> x7, waiting for transfers between devices: 55.8 us -> 307 us  [the longest x3 203 us: shards(): lax.all_gather(basis_rows.astype(jnp.bfloat16), 'col', axis=0, tiled=True)]
    psum x6 -> x3, waiting for transfers between devices: 604 us -> 378 us  [orthonormal(): gram = lax.psum(partial_gram, ('grad', 'col'))]
    reshape x0 -> x2, local copies, waits for them, and re-layouts: none -> 110 us  [shards(): split = gradient.reshape(n_rows, n_col, n_grad, piece)]
    all_to_all x1 -> x0, local copies, waits for them, and re-layouts: 64.6 us -> none  [shards(): lax.all_to_all(gradient, 'col', split_axis=1, concat_axis=0, tiled=True)]
    unnamed x15 -> x9, local copies, waits for them, and re-layouts: 82.9 us -> 46.8 us
    reduce_scatter x3, waiting for transfers between devices: 134 us -> 97.7 us  [shards(): lax.psum_scatter(jnp.dot(blocks, basis_bf, preferred_element_type=jnp.flo...]
  transfers between devices with their start and end apart: 13 -> 17, of which waited for: 12 -> 16; matrix products, arithmetic and copies ran while one was open for 3% -> 3% of each run, Pallas kernels for 0% -> 0%
where the time goes in v1:
time: 2370 us; the launch traced here: 2360 us
  waiting for transfers between devices  1800 us (76%)
  matrix products  184 us (8%)
  other arithmetic  173 us (7%)
  local copies, waits for them, and re-layouts  172 us (7%)
    all_to_all x1, waiting for transfers between devices, shards(): lax.all_to_all(split, 'grad', split_axis=2, concat_axis=0, tiled=True)  596 us
    reduce_scatter x3, waiting for transfers between devices, sketch_of(): return lax.psum_scatter(partial, 'col', scatter_dimension=0, tiled=True)  417 us
    psum x3, waiting for transfers between devices, orthonormal(): gram = lax.psum(partial_gram, ('grad', 'col'))  378 us
    all_gather x3, waiting for transfers between devices, shards(): lax.all_gather(basis_rows.astype(jnp.bfloat16), 'col', axis=0, tiled=True)  203 us
    reshape x2, local copies, waits for them, and re-layouts, shards(): split = gradient.reshape(n_rows, n_col, n_grad, piece)  110 us
    another operation x20, other arithmetic, orthonormal(): lower_factor = jnp.linalg.cholesky(gram)  103 us
    reduce_scatter x3, waiting for transfers between devices, shards(): lax.psum_scatter(jnp.dot(blocks, basis_bf, preferred_element_type=jnp.flo...  97.7 us
    dot_general x3, matrix products, sketch_of(): lax.dot_general(blocks, rows, (((0,), (0,)), ((), ())), preferred_element...  84.8 us
  transfers between devices with their start and end apart: 17, of which 16 were waited for; matrix products, arithmetic and copies ran while one was open for 3% of the time, Pallas kernels for 0%

profile of v1, /device:TPU:0, one launch (start us, length us, event | category | flops | bytes accessed | tf_op | source)
XLA Modules:
  0.0 2358.3 jit_solution(13075918259095874959)
XLA Ops:
  7.2 73.2 %reshape.28 = bf16[512,8,4,1664]{3,2,1,0:T(4,128)(2,1)} reshape(bf16[512,53248]{1,0:T(8,128)(2,1)} %param.5) | data formatting | bytes 109051904 | tf_op jit(solution)/shard_map/reshape | solution.py:32
  80.4 36.6 %copy.12 = bf16[512,8,4,1664]{3,1,0,2:T(8,128)(2,1)} copy(bf16[512,8,4,1664]{3,2,1,0:T(4,128)(2,1)} %reshape.28) | data formatting | bytes 109051904 | tf_op jit(solution)/shard_map/reshape | solution.py:32
  117.0 12.1 all-to-all-start
  129.8 596.0 %all-to-all-done = bf16[512,8,4,1664]{3,1,0,2:T(8,128)(2,1)} async-done(((bf16[512,8,4,1664]{3,1,0,2:T(8,128)(2,1)}), bf16[512,8,4,1664]{3,1,0,2:T(8,128)(2,1)}, u32[]{:S(2)}, u32[]{:S(2)}) %all-to-all-start) | async-done | bytes 54525984 | tf_op jit(solution)/shard_map/all_to_all | solution.py:33
  725.8 36.6 %copy.24 = bf16[256,8,8,1664]{3,1,2,0:T(8,128)(2,1)} copy(bf16[256,8,8,1664]{3,2,1,0:T(8,128)(2,1)} %bitcast.37) | data formatting | bytes 109051904
  762.4 28.2 %fusion.37 = f32[13312,256]{1,0:T(8,128)} fusion(bf16[2048,13312]{1,0:T(8,128)(2,1)} %bitcast.131, bf16[2048,256]{1,0:T(8,128)(2,1)} %all-gather.8.cloned.1.call-done), kind=kOutput, calls=%fused_computation.90 | convolution fusion | flops 13958643712 | bytes 69206016 | tf_op jit(solution)/shard_map/dot_general | solution.py:38
  790.7 139.5 %reduce-scatter.7.cloned.1.call-done = f32[1664,256]{1,0:T(8,128)} async-done(((f32[13312,256]{1,0:T(8,128)}), f32[1664,256]{1,0:T(8,128)}) %reduce-scatter.7.cloned.1.call-update) | async-done | bytes 1703952 | tf_op jit(solution)/shard_map/reduce_scatter | solution.py:41
  930.2 5.9 fusion.38
  936.3 125.0 %all-reduce.5.cloned.1.call-done = f32[256,256]{0,1:T(8,128)} async-done(((f32[256,256]{0,1:T(8,128)}), f32[256,256]{0,1:T(8,128)}) %all-reduce.5.cloned.1.call-update) | async-done | bytes 262160 | tf_op jit(solution)/shard_map/psum | solution.py:20
  1061.3 1.1 copy.14
  1062.4 1.0 fusion.10
  1063.4 11.7 cholesky.172
  1075.2 9.8 custom-call.15
  1085.5 11.7 cholesky.189
  1099.3 4.2 while.6
  1100.1 1.4 bitcast_dynamic-update-slice_fusion.6
  1102.1 1.4 bitcast_dynamic-update-slice_fusion.6
  1103.5 19.7 custom-call.16
  1124.2 1.5 convolution_subtract_fusion.2
  1126.7 1.0 maximum_convert_fusion
  1127.7 68.2 %all-gather.10.cloned.1.call-done = bf16[13312,256]{0,1:T(8,128)(2,1)} async-done(((bf16[1664,256]{0,1:T(8,128)(2,1)}), bf16[13312,256]{0,1:T(8,128)(2,1)}) %all-gather.10.cloned.1.call-update) | async-done | bytes 6815760 | tf_op jit(solution)/shard_map/all_gather | solution.py:46
  1195.9 24.2 %convolution_bitcast_fusion.4 = f32[2048,256]{0,1:T(8,128)} fusion(bf16[13312,256]{0,1:T(8,128)(2,1)} %all-gather.10.cloned.1.call-done, bf16[2048,13312]{1,0:T(8,128)(2,1)} %bitcast.132), kind=kOutput, calls=%fused_computation.10 | convolution fusion | flops 13958643712 | bytes 63438848 | tf_op jit(solution)/shard_map/dot_general | solution.py:48
  1220.2 33.9 %reduce-scatter.9.cloned.1.call-done = f32[512,256]{0,1:T(8,128)} async-done(((f32[2048,256]{0,1:T(8,128)}), f32[512,256]{0,1:T(8,128)}) %reduce-scatter.9.cloned.1.call-update) | async-done | bytes 524304 | tf_op jit(solution)/shard_map/reduce_scatter | solution.py:47
  1254.1 1.8 convert_element_type.16
  1255.9 26.8 %all-gather.12.cloned.1.call-done = bf16[2048,256]{0,1:T(8,128)(2,1)} async-done(((bf16[512,256]{0,1:T(8,128)(2,1)}), bf16[2048,256]{0,1:T(8,128)(2,1)}) %all-gather.12.cloned.1.call-update) | async-done | bytes 1048592 | tf_op jit(solution)/shard_map/all_gather | solution.py:37
  1282.8 28.3 %convolution_bitcast_fusion.1 = f32[13312,256]{0,1:T(8,128)} fusion(bf16[2048,256]{0,1:T(8,128)(2,1)} %all-gather.12.cloned.1.call-done, bf16[2048,13312]{1,0:T(8,128)(2,1)} %bitcast.133), kind=kOutput, calls=%fused_computation.7 | convolution fusion | flops 13958643712 | bytes 69206016 | tf_op jit(solution)/shard_map/dot_general | solution.py:38
  1311.6 138.7 %reduce-scatter.11.cloned.1.call-done = f32[1664,256]{0,1:T(8,128)} async-done(((f32[13312,256]{0,1:T(8,128)}), f32[1664,256]{0,1:T(8,128)}) %reduce-scatter.11.cloned.1.call-update) | async-done | bytes 1703952 | tf_op jit(solution)/shard_map/reduce_scatter | solution.py:41
  1450.3 4.7 fusion.39
  1455.0 126.4 %all-reduce.7.cloned.1.call-done = f32[256,256]{0,1:T(8,128)} async-done(((f32[256,256]{0,1:T(8,128)}), f32[256,256]{0,1:T(8,128)}) %all-reduce.7.cloned.1.call-update) | async-done | bytes 262160 | tf_op jit(solution)/shard_map/psum | solution.py:20
  1581.4 1.1 copy.16
  1582.5 1.0 fusion.9
  1583.5 11.7 cholesky.206
  1595.3 9.8 custom-call.17
  1605.6 11.7 cholesky.223
  1620.0 4.1 while.7
  1620.8 1.4 bitcast_dynamic-update-slice_fusion.7
  1622.8 1.4 bitcast_dynamic-update-slice_fusion.7
  1624.1 19.7 custom-call.18
  1647.6 68.2 %all-gather.14.cloned.1.call-done = bf16[13312,256]{0,1:T(8,128)(2,1)} async-done(((bf16[1664,256]{0,1:T(8,128)(2,1)}), bf16[13312,256]{0,1:T(8,128)(2,1)}) %all-gather.14.cloned.1.call-update) | async-done | bytes 6815760 | tf_op jit(solution)/shard_map/all_gather | solution.py:46
  1715.8 24.2 %convolution_bitcast_fusion.3 = f32[2048,256]{0,1:T(8,128)} fusion(bf16[13312,256]{0,1:T(8,128)(2,1)} %all-gather.14.cloned.1.call-done, bf16[2048,13312]{1,0:T(8,128)(2,1)} %bitcast.134), kind=kOutput, calls=%fused_computation.9 | convolution fusion | flops 13958643712 | bytes 63438848 | tf_op jit(solution)/shard_map/dot_general | solution.py:48
  1740.1 33.9 %reduce-scatter.13.cloned.1.call-done = f32[512,256]{0,1:T(8,128)} async-done(((f32[2048,256]{0,1:T(8,128)}), f32[512,256]{0,1:T(8,128)}) %reduce-scatter.13.cloned.1.call-update) | async-done | bytes 524304 | tf_op jit(solution)/shard_map/reduce_scatter | solution.py:47
  1774.0 1.8 convert_element_type.18
  1775.8 27.0 %all-gather.16.cloned.1.call-done = bf16[2048,256]{0,1:T(8,128)(2,1)} async-done(((bf16[512,256]{0,1:T(8,128)(2,1)}), bf16[2048,256]{0,1:T(8,128)(2,1)}) %all-gather.16.cloned.1.call-update) | async-done | bytes 1048592 | tf_op jit(solution)/shard_map/all_gather | solution.py:37
  1802.8 28.3 %convolution_bitcast_fusion = f32[13312,256]{0,1:T(8,128)} fusion(bf16[2048,256]{0,1:T(8,128)(2,1)} %all-gather.16.cloned.1.call-done, bf16[2048,13312]{1,0:T(8,128)(2,1)} %bitcast.135), kind=kOutput, calls=%fused_computation.6 | convolution fusion | flops 13958643712 | bytes 69206016 | tf_op jit(solution)/shard_map/dot_general | solution.py:38
  1831.4 138.9 %reduce-scatter.15.cloned.1.call-done = f32[1664,256]{0,1:T(8,128)} async-done(((f32[13312,256]{0,1:T(8,128)}), f32[1664,256]{0,1:T(8,128)}) %reduce-scatter.15.cloned.1.call-update) | async-done | bytes 1703952 | tf_op jit(solution)/shard_map/reduce_scatter | solution.py:41
  1970.3 4.7 fusion.40
  1975.1 126.4 %all-reduce.9.cloned.1.call-done = f32[256,256]{0,1:T(8,128)} async-done(((f32[256,256]{0,1:T(8,128)}), f32[256,256]{0,1:T(8,128)}) %all-reduce.9.cloned.1.call-update) | async-done | bytes 262160 | tf_op jit(solution)/shard_map/psum | solution.py:20
  2101.5 1.1 copy.18
  2102.6 1.0 fusion.8
  2103.6 11.7 cholesky.240
  2115.3 9.8 custom-call.19
  2125.6 11.7 cholesky.257
  2140.0 4.3 while.8
  2140.9 1.4 bitcast_dynamic-update-slice_fusion.8
  2142.9 1.4 bitcast_dynamic-update-slice_fusion.8
  2144.3 19.7 custom-call.20
  2166.7 1.0 fusion.1
  2167.8 1.3 fusion
  2169.2 66.8 %all-gather.18.cloned.1.call-done = bf16[13312,256]{0,1:T(8,128)(2,1)} async-done(((bf16[1664,256]{0,1:T(8,128)(2,1)}), bf16[13312,256]{0,1:T(8,128)(2,1)}) %all-gather.18.cloned.1.call-update) | async-done | bytes 6815760 | tf_op jit(solution)/shard_map/all_gather | solution.py:46
  2236.0 25.5 %convolution_bitcast_fusion.2 = f32[2048,256]{0,1:T(8,128)} fusion(bf16[13312,256]{0,1:T(8,128)(2,1)} %all-gather.18.cloned.1.call-done, bf16[2048,13312]{1,0:T(8,128)(2,1)} %bitcast.136), kind=kOutput, calls=%fused_computation.8 | convolution fusion | flops 13958643712 | bytes 63438848 | tf_op jit(solution)/shard_map/dot_general | solution.py:48
  2261.5 49.8 %all-gather.20.cloned.1.call-done = f32[6656,256]{0,1:T(8,128)} async-done(((f32[1664,256]{0,1:T(8,128)}), f32[6656,256]{0,1:T(8,128)}) %all-gather.20.cloned.1.call-update) | async-done | bytes 6815760 | tf_op jit(solution)/shard_map/all_gather | solution.py:55
  2311.3 8.1 copy.20
  2319.3 30.0 %reduce-scatter.17.cloned.1.call-done = f32[512,256]{0,1:T(8,128)} async-done(((f32[2048,256]{0,1:T(8,128)}), f32[512,256]{0,1:T(8,128)}) %reduce-scatter.17.cloned.1.call-update) | async-done | bytes 524304 | tf_op jit(solution)/shard_map/reduce_scatter | solution.py:47
  2349.3 2.0 copy.19
  (91 shorter events, 19.4 us)
Async XLA Ops:
  117.0 608.8 %all-to-all-start = ((bf16[512,8,4,1664]{3,1,0,2:T(8,128)(2,1)}), bf16[512,8,4,1664]{3,1,0,2:T(8,128)(2,1)}, u32[]{:S(2)}, u32[]{:S(2)}) async-start(bf16[512,8,4,1664]{3,1,0,2:T(8,128)(2,1)} %copy.12), calls=%async_computation | async-start | bytes 109051904 | tf_op jit(solution)/shard_map/all_to_all | solution.py:33
  129.0 633.4 %all-gather.8.cloned.1.call-start = ((), (), s32[]{:S(2)}) async-start(), calls=%async_computation.7 | async-start | bytes 1310720 | tf_op jit(solution)/shard_map/all_gather | solution.py:37
  129.8 800.4 %reduce-scatter.7.cloned.1.call-start = ((), (), s32[]{:S(2)}) async-start(), calls=%async_computation.8 | async-start | bytes 15335424 | tf_op jit(solution)/shard_map/reduce_scatter | solution.py:41
  790.6 270.7 %all-reduce.5.cloned.1.call-start = ((), (), s32[]{:S(2)}) async-start(), calls=%async_computation.9 | async-start | bytes 524288 | tf_op jit(solution)/shard_map/psum | solution.py:20
  936.1 187.1 %copy-start = (f32[1664,256]{1,0:T(8,128)S(1)}, f32[1664,256]{1,0:T(8,128)}, u32[]{:S(2)}) copy-start(f32[1664,256]{1,0:T(8,128)} %reduce-scatter.7.cloned.1.call-done) | copy-start | bytes 5111812
  936.1 259.8 %all-gather.10.cloned.1.call-start = ((), (), s32[]{:S(2)}) async-start(), calls=%async_computation.10 | async-start | bytes 7667712 | tf_op jit(solution)/shard_map/all_gather | solution.py:46
  1127.7 126.4 %reduce-scatter.9.cloned.1.call-start = ((), (), s32[]{:S(2)}) async-start(), calls=%async_computation.11 | async-start | bytes 2621440 | tf_op jit(solution)/shard_map/reduce_scatter | solution.py:47
  1220.2 62.6 %all-gather.12.cloned.1.call-start = ((), (), s32[]{:S(2)}) async-start(), calls=%async_computation.12 | async-start | bytes 1310720 | tf_op jit(solution)/shard_map/all_gather | solution.py:37
  1255.9 194.4 %reduce-scatter.11.cloned.1.call-start = ((), (), s32[]{:S(2)}) async-start(), calls=%async_computation.13 | async-start | bytes 15335424 | tf_op jit(solution)/shard_map/reduce_scatter | solution.py:41
  1311.1 270.3 %all-reduce.7.cloned.1.call-start = ((), (), s32[]{:S(2)}) async-start(), calls=%async_computation.14 | async-start | bytes 524288 | tf_op jit(solution)/shard_map/psum | solution.py:20
  1455.0 188.8 %copy-start.2 = (f32[1664,256]{0,1:T(8,128)S(1)}, f32[1664,256]{0,1:T(8,128)}, u32[]{:S(2)}) copy-start(f32[1664,256]{0,1:T(8,128)} %reduce-scatter.11.cloned.1.call-done) | copy-start | bytes 5111812
  1455.0 260.8 %all-gather.14.cloned.1.call-start = ((), (), s32[]{:S(2)}) async-start(), calls=%async_computation.15 | async-start | bytes 7667712 | tf_op jit(solution)/shard_map/all_gather | solution.py:46
  1647.6 126.4 %reduce-scatter.13.cloned.1.call-start = ((), (), s32[]{:S(2)}) async-start(), calls=%async_computation.16 | async-start | bytes 2621440 | tf_op jit(solution)/shard_map/reduce_scatter | solution.py:47
  1740.0 62.8 %all-gather.16.cloned.1.call-start = ((), (), s32[]{:S(2)}) async-start(), calls=%async_computation.17 | async-start | bytes 1310720 | tf_op jit(solution)/shard_map/all_gather | solution.py:37
  1775.8 194.6 %reduce-scatter.15.cloned.1.call-start = ((), (), s32[]{:S(2)}) async-start(), calls=%async_computation.18 | async-start | bytes 15335424 | tf_op jit(solution)/shard_map/reduce_scatter | solution.py:41
  1831.2 270.3 %all-reduce.9.cloned.1.call-start = ((), (), s32[]{:S(2)}) async-start(), calls=%async_computation.19 | async-start | bytes 524288 | tf_op jit(solution)/shard_map/psum | solution.py:20
  1975.0 188.9 %copy-start.1 = (f32[1664,256]{0,1:T(8,128)S(1)}, f32[1664,256]{0,1:T(8,128)}, u32[]{:S(2)}) copy-start(f32[1664,256]{0,1:T(8,128)} %reduce-scatter.15.cloned.1.call-done) | copy-start | bytes 5111812
  1975.0 260.9 %all-gather.18.cloned.1.call-start = ((), (), s32[]{:S(2)}) async-start(), calls=%async_computation.20 | async-start | bytes 7667712 | tf_op jit(solution)/shard_map/all_gather | solution.py:46
  2167.7 143.5 %all-gather.20.cloned.1.call-start = ((), (), s32[]{:S(2)}) async-start(), calls=%async_computation.22 | async-start | bytes 8519680 | tf_op jit(solution)/shard_map/all_gather | solution.py:55
  2169.1 180.2 %reduce-scatter.17.cloned.1.call-start = ((), (), s32[]{:S(2)}) async-start(), calls=%async_computation.21 | async-start | bytes 2621440 | tf_op jit(solution)/shard_map/reduce_scatter | solution.py:47
Sparse Core Ops, SparseCore 0:
  131.7 318.6 all-gather.7
  790.8 139.4 reduce-scatter.6
  936.3 124.9 all-reduce.4
  1127.8 68.0 all-gather.9
  1220.3 33.7 reduce-scatter.8
  1256.3 26.3 all-gather.11
  1311.2 139.0 reduce-scatter.10
  1456.4 125.0 all-reduce.6
  1647.7 68.0 all-gather.13
  1740.2 33.7 reduce-scatter.12
  1776.4 26.3 all-gather.15
  1831.3 139.0 reduce-scatter.14
  1976.4 125.0 all-reduce.8
  2167.9 68.0 all-gather.17
  2238.2 72.9 all-gather.19
  2314.1 35.1 reduce-scatter.16

commit v2 on v1

v2 whole, which is shorter than its diff:
```python
import math

import jax
import jax.numpy as jnp
from jax import lax
from jax.sharding import PartitionSpec as P

FF = 53248
POWER = 2
HALVES = 2


def all_sum(value, axes):
    for axis in axes:
        size = lax.axis_size(axis)
        if size & (size - 1):
            value = lax.psum(value, axis)
            continue
        step = 1
        while step < size:
            value = value + lax.ppermute(value, axis, [(i, i ^ step) for i in range(size)])
            step *= 2
    return value


def orthonormal(rows):
    partial_gram = lax.dot_general(
        rows,
        rows,
        (((0,), (0,)), ((), ())),
        precision=lax.Precision.HIGHEST,
        preferred_element_type=jnp.float32,
    )
    gram = all_sum(partial_gram, ("col", "grad"))
    lower_factor = jnp.linalg.cholesky(gram)
    return lax.linalg.triangular_solve(
        lower_factor, rows, left_side=False, lower=True, transpose_a=True
    )


def shards(gradient, test_matrix):
    n_grad = lax.axis_size("grad")
    n_col = lax.axis_size("col")
    n_rows, n_ff = gradient.shape
    piece = n_ff // (n_col * n_grad)
    half = piece // HALVES
    split = gradient.reshape(n_rows, n_col, n_grad, HALVES, half)
    chunks = []
    for h in range(HALVES):
        moved = lax.all_to_all(split[:, :, :, h], "grad", split_axis=2, concat_axis=0, tiled=True)
        chunks.append(moved.reshape(n_grad * n_rows, n_col * half))

    def sketch_of(row_piece):
        rows = lax.all_gather(row_piece, "grad", axis=0, tiled=True)
        parts = []
        for chunk in chunks:
            partial = lax.dot_general(
                chunk, rows, (((0,), (0,)), ((), ())), preferred_element_type=jnp.float32
            )
            parts.append(lax.psum_scatter(partial, "col", scatter_dimension=0, tiled=True))
        return jnp.concatenate(parts, axis=0)

    sketch = sketch_of(test_matrix)
    for iteration in range(POWER + 1):
        basis_rows = orthonormal(sketch)
        basis_bf = lax.all_gather(
            basis_rows.astype(jnp.bfloat16).reshape(HALVES, half, -1), "col", axis=1, tiled=True
        )
        partial = jnp.dot(chunks[0], basis_bf[0], preferred_element_type=jnp.float32)
        for h in range(1, HALVES):
            partial = partial + jnp.dot(chunks[h], basis_bf[h], preferred_element_type=jnp.float32)
        reduced = lax.psum_scatter(partial, "grad", scatter_dimension=0, tiled=True)
        if iteration < POWER:
            sketch = sketch_of(reduced.astype(jnp.bfloat16))
    projector = lax.all_gather(basis_rows * math.sqrt(FF), "grad", axis=0, tiled=True)
    return (reduced, projector)


def solution(mesh):
    return jax.shard_map(
        shards,
        mesh=mesh,
        in_specs=(P(("grad", "col"), None), P(("grad", "col"), None)),
        out_specs=(P(("grad", "col"), None), P("col", None)),
        check_vma=False,
    )
```

time: 2370 us -> 2100 us (0.89)
  waiting for transfers between devices: 1800 us -> 1360 us
  local copies, waits for them, and re-layouts: 172 us -> 313 us
    psum x3 -> x0, waiting for transfers between devices: 378 us -> none  [orthonormal(): gram = lax.psum(partial_gram, ('grad', 'col'))]
    all_to_all x1 -> x2, waiting for transfers between devices: 596 us -> 392 us  [shards(): lax.all_to_all(split[:, :, :, h], 'grad', split_axis=2, concat_axis=0, ti...]
    all_gather x3, waiting for transfers between devices: 53.8 us -> 176 us  [sketch_of(): rows = lax.all_gather(row_piece, 'grad', axis=0, tiled=True)]
    unnamed x9 -> x24, local copies, waits for them, and re-layouts: 46.8 us -> 157 us
    reshape x2 -> x0, local copies, waits for them, and re-layouts: 110 us -> none  [shards(): split = gradient.reshape(n_rows, n_col, n_grad, piece)]
    ppermute x0 -> x15, waiting for transfers between devices: none -> 108 us  [all_sum(): lax.ppermute(value, axis, [(i, i ^ step) for i in range(size)])]
    squeeze x0 -> x3, local copies, waits for them, and re-layouts: none -> 73.1 us  [shards(): split[:, :, :, h]]
    reduce_scatter x6 -> x9, waiting for transfers between devices: 515 us -> 442 us  [the longest x6 345 us: sketch_of(): lax.psum_scatter(partial, 'col', scatter_dimension=0, tiled=True)]
  transfers between devices with their start and end apart: 17 -> 33, of which waited for: 16 -> 33; matrix products, arithmetic and copies ran while one was open for 3% -> 11% of each run, Pallas kernels for 0% -> 0%
where the time goes in v2:
time: 2100 us; the launch traced here: 2090 us
  waiting for transfers between devices  1360 us (65%)
  local copies, waits for them, and re-layouts  313 us (15%)
  matrix products  196 us (9%)
  other arithmetic  169 us (8%)
  starting transfers between devices  31.8 us (2%)
    all_to_all x2, waiting for transfers between devices, shards(): lax.all_to_all(split[:, :, :, h], 'grad', split_axis=2, concat_axis=0, ti...  392 us
    reduce_scatter x6, waiting for transfers between devices, sketch_of(): lax.psum_scatter(partial, 'col', scatter_dimension=0, tiled=True)  345 us
    all_gather x3, waiting for transfers between devices, shards(): lax.all_gather(basis_rows.astype(jnp.bfloat16).reshape(HALVES, half, -1),...  199 us
    all_gather x3, waiting for transfers between devices, sketch_of(): rows = lax.all_gather(row_piece, 'grad', axis=0, tiled=True)  176 us
    unnamed x24, local copies, waits for them, and re-layouts  157 us
    ppermute x15, waiting for transfers between devices, all_sum(): lax.ppermute(value, axis, [(i, i ^ step) for i in range(size)])  108 us
    another operation x20, other arithmetic, orthonormal(): lower_factor = jnp.linalg.cholesky(gram)  104 us
    reduce_scatter x3, waiting for transfers between devices, shards(): reduced = lax.psum_scatter(partial, 'grad', scatter_dimension=0, tiled=True)  97.7 us
  transfers between devices with their start and end apart: 33, of which 33 were waited for; matrix products, arithmetic and copies ran while one was open for 11% of the time, Pallas kernels for 0%

profile of v2, /device:TPU:0, one launch (start us, length us, event | category | flops | bytes accessed | tf_op | source)
XLA Modules:
  0.0 2092.2 jit_solution(2185599486766137537)
XLA Ops:
  7.2 70.4 %copy.32 = bf16[512,53248]{0,1:T(8,128)(2,1)} copy(bf16[512,53248]{1,0:T(8,128)(2,1)} %param.5) | data formatting | bytes 109051904 | tf_op args[0]
  77.6 35.6 %slice_bitcast_fusion.1 = (bf16[512,8,4,832]{0,3,2,1:T(8,128)(2,1)}, bf16[512,8,4,832]{0,3,2,1:T(8,128)(2,1)}) fusion(bf16[512,8,4,2,832]{0,4,3,2,1:T(8,128)(2,1)} %bitcast.204), kind=kLoop, calls=%fused_computation.7 | loop fusion | bytes 109051904 | tf_op jit(solution)/shard_map/squeeze | solution.py:50
  113.2 18.8 copy.33
  132.0 8.8 all-to-all-start
  140.8 18.7 copy.35
  159.5 277.4 %all-to-all-done = bf16[512,8,4,832]{0,3,1,2:T(8,128)(2,1)} async-done(((bf16[512,8,4,832]{0,3,1,2:T(8,128)(2,1)}), bf16[512,8,4,832]{0,3,1,2:T(8,128)(2,1)}, u32[]{:S(2)}, u32[]{:S(2)}) %all-to-all-start) | async-done | bytes 27263008 | tf_op jit(solution)/shard_map/all_to_all | solution.py:50
  436.9 8.7 all-to-all-start.1
  446.4 31.4 %copy.34 = bf16[4,512,8,1,832]{1,0,4,2,3:T(4,128)(2,1)} copy(bf16[4,512,8,1,832]{1,4,2,0,3:T(8,128)(2,1)} %bitcast.3) | data formatting | bytes 54525952 | tf_op jit(solution)/shard_map/all_to_all | solution.py:50
  477.8 19.0 copy.66
  496.8 122.1 %all-gather.8.cloned.1.call-done = bf16[2048,256]{1,0:T(8,128)(2,1)} async-done(((bf16[512,256]{1,0:T(8,128)(2,1)}), bf16[2048,256]{1,0:T(8,128)(2,1)}) %all-gather.8.cloned.1.call-update) | async-done | bytes 1048592 | tf_op jit(solution)/shard_map/all_gather | solution.py:54
  618.9 14.5 fusion.49
  634.0 114.3 %all-to-all-done.1 = bf16[512,8,4,832]{0,3,1,2:T(8,128)(2,1)} async-done(((bf16[512,8,4,832]{0,3,1,2:T(8,128)(2,1)}), bf16[512,8,4,832]{0,3,1,2:T(8,128)(2,1)}, u32[]{:S(2)}, u32[]{:S(2)}) %all-to-all-start.1) | async-done | bytes 27263008 | tf_op jit(solution)/shard_map/all_to_all | solution.py:50
  748.4 31.4 %copy.36 = bf16[4,512,8,1,832]{1,0,4,2,3:T(4,128)(2,1)} copy(bf16[4,512,8,1,832]{1,4,2,0,3:T(8,128)(2,1)} %bitcast.6) | data formatting | bytes 54525952 | tf_op jit(solution)/shard_map/all_to_all | solution.py:50
  779.7 19.4 copy.67
  799.1 15.5 fusion.50
  814.8 23.3 %reduce-scatter.18.cloned.1.call-done = f32[832,256]{1,0:T(8,128)} async-done(((f32[6656,256]{1,0:T(8,128)}), f32[832,256]{1,0:T(8,128)}) %reduce-scatter.18.cloned.1.call-update) | async-done | bytes 851984 | tf_op jit(solution)/shard_map/reduce_scatter | solution.py:60
  839.4 74.3 %reduce-scatter.20.cloned.1.call-done = f32[832,256]{1,0:T(8,128)} async-done(((f32[6656,256]{1,0:T(8,128)}), f32[832,256]{1,0:T(8,128)}) %reduce-scatter.20.cloned.1.call-update) | async-done | bytes 851984 | tf_op jit(solution)/shard_map/reduce_scatter | solution.py:60
  919.4 8.3 collective-permute-done.1
  928.4 13.4 collective-permute-done.2
  943.4 6.8 collective-permute-done.3
  957.9 11.7 cholesky.172
  969.7 9.8 custom-call.15
  980.0 11.9 cholesky.189
  998.0 19.7 custom-call.16
  1022.9 66.9 %all-gather.10.cloned.1.call-done = bf16[2,6656,256]{2,1,0:T(8,128)(2,1)} async-done(((bf16[2,832,256]{2,1,0:T(8,128)(2,1)}), bf16[2,6656,256]{2,1,0:T(8,128)(2,1)}) %all-gather.10.cloned.1.call-update) | async-done | bytes 6815760 | tf_op jit(solution)/shard_map/all_gather | solution.py:66
  1089.8 13.6 fusion.4
  1103.4 14.0 fusion.7
  1117.5 33.9 %reduce-scatter.22.cloned.1.call-done = f32[512,256]{0,1:T(8,128)} async-done(((f32[2048,256]{0,1:T(8,128)}), f32[512,256]{0,1:T(8,128)}) %reduce-scatter.22.cloned.1.call-update) | async-done | bytes 524304 | tf_op jit(solution)/shard_map/reduce_scatter | solution.py:72
  1153.3 26.8 %all-gather.12.cloned.1.call-done = bf16[2048,256]{0,1:T(8,128)(2,1)} async-done(((bf16[512,256]{0,1:T(8,128)(2,1)}), bf16[2048,256]{0,1:T(8,128)(2,1)}) %all-gather.12.cloned.1.call-update) | async-done | bytes 1048592 | tf_op jit(solution)/shard_map/all_gather | solution.py:54
  1180.1 14.5 convolution_bitcast_fusion.3
  1194.6 8.1 copy.58
  1204.0 16.0 convolution_bitcast_fusion.2
  1219.9 8.2 copy.60
  1228.4 49.2 %reduce-scatter.28.cloned.1.call-done = f32[832,256]{1,0:T(8,128)} async-done(((f32[6656,256]{1,0:T(8,128)}), f32[832,256]{1,0:T(8,128)}) %reduce-scatter.28.cloned.1.call-update) | async-done | bytes 851984 | tf_op jit(solution)/shard_map/reduce_scatter | solution.py:60
  1278.8 74.3 %reduce-scatter.30.cloned.1.call-done = f32[832,256]{1,0:T(8,128)} async-done(((f32[6656,256]{1,0:T(8,128)}), f32[832,256]{1,0:T(8,128)}) %reduce-scatter.30.cloned.1.call-update) | async-done | bytes 851984 | tf_op jit(solution)/shard_map/reduce_scatter | solution.py:60
  1358.9 8.3 collective-permute-done.6
  1367.9 13.4 collective-permute-done.7
  1397.3 11.7 cholesky.206
  1409.1 9.8 custom-call.17
  1419.4 11.9 cholesky.223
  1438.0 19.7 custom-call.18
  1463.0 66.9 %all-gather.14.cloned.1.call-done = bf16[2,6656,256]{2,1,0:T(8,128)(2,1)} async-done(((bf16[2,832,256]{2,1,0:T(8,128)(2,1)}), bf16[2,6656,256]{2,1,0:T(8,128)(2,1)}) %all-gather.14.cloned.1.call-update) | async-done | bytes 6815760 | tf_op jit(solution)/shard_map/all_gather | solution.py:66
  1529.8 13.6 fusion.2
  1543.4 14.0 fusion.9
  1557.6 33.9 %reduce-scatter.24.cloned.1.call-done = f32[512,256]{0,1:T(8,128)} async-done(((f32[2048,256]{0,1:T(8,128)}), f32[512,256]{0,1:T(8,128)}) %reduce-scatter.24.cloned.1.call-update) | async-done | bytes 524304 | tf_op jit(solution)/shard_map/reduce_scatter | solution.py:72
  1593.3 27.0 %all-gather.16.cloned.1.call-done = bf16[2048,256]{0,1:T(8,128)(2,1)} async-done(((bf16[512,256]{0,1:T(8,128)(2,1)}), bf16[2048,256]{0,1:T(8,128)(2,1)}) %all-gather.16.cloned.1.call-update) | async-done | bytes 1048592 | tf_op jit(solution)/shard_map/all_gather | solution.py:54
  1620.3 14.5 convolution_bitcast_fusion.1
  1634.8 8.1 copy.62
  1644.1 16.0 convolution_bitcast_fusion
  1660.1 8.2 copy.64
  1668.5 49.2 %reduce-scatter.32.cloned.1.call-done = f32[832,256]{1,0:T(8,128)} async-done(((f32[6656,256]{1,0:T(8,128)}), f32[832,256]{1,0:T(8,128)}) %reduce-scatter.32.cloned.1.call-update) | async-done | bytes 851984 | tf_op jit(solution)/shard_map/reduce_scatter | solution.py:60
  1719.0 74.3 %reduce-scatter.34.cloned.1.call-done = f32[832,256]{1,0:T(8,128)} async-done(((f32[6656,256]{1,0:T(8,128)}), f32[832,256]{1,0:T(8,128)}) %reduce-scatter.34.cloned.1.call-update) | async-done | bytes 851984 | tf_op jit(solution)/shard_map/reduce_scatter | solution.py:60
  1799.0 8.3 collective-permute-done.11
  1808.0 13.4 collective-permute-done.12
  1837.5 11.7 cholesky.240
  1849.3 9.8 custom-call.19
  1859.6 11.9 cholesky.257
  1878.2 19.7 custom-call.20
  1904.4 65.6 %all-gather.18.cloned.1.call-done = bf16[2,6656,256]{2,1,0:T(8,128)(2,1)} async-done(((bf16[2,832,256]{2,1,0:T(8,128)(2,1)}), bf16[2,6656,256]{2,1,0:T(8,128)(2,1)}) %all-gather.18.cloned.1.call-update) | async-done | bytes 6815760 | tf_op jit(solution)/shard_map/all_gather | solution.py:66
  1970.0 14.8 fusion
  1984.9 14.1 fusion.11
  1999.0 46.4 %all-gather.20.cloned.1.call-done = f32[6656,256]{0,1:T(8,128)} async-done(((f32[1664,256]{0,1:T(8,128)}), f32[6656,256]{0,1:T(8,128)}) %all-gather.20.cloned.1.call-update) | async-done | bytes 6815760 | tf_op jit(solution)/shard_map/all_gather | solution.py:75
  2045.3 8.1 copy.54
  2053.4 30.0 %reduce-scatter.26.cloned.1.call-done = f32[512,256]{0,1:T(8,128)} async-done(((f32[2048,256]{0,1:T(8,128)}), f32[512,256]{0,1:T(8,128)}) %reduce-scatter.26.cloned.1.call-update) | async-done | bytes 524304 | tf_op jit(solution)/shard_map/reduce_scatter | solution.py:72
  (168 shorter events, 120.3 us)
Async XLA Ops:
  132.0 304.9 %all-to-all-start = ((bf16[512,8,4,832]{0,3,1,2:T(8,128)(2,1)}), bf16[512,8,4,832]{0,3,1,2:T(8,128)(2,1)}, u32[]{:S(2)}, u32[]{:S(2)}) async-start(bf16[512,8,4,832]{0,3,1,2:T(8,128)(2,1)} %copy.33), calls=%async_computation | async-start | bytes 54525952 | tf_op jit(solution)/shard_map/all_to_all | solution.py:50
  436.9 311.4 %all-to-all-start.1 = ((bf16[512,8,4,832]{0,3,1,2:T(8,128)(2,1)}), bf16[512,8,4,832]{0,3,1,2:T(8,128)(2,1)}, u32[]{:S(2)}, u32[]{:S(2)}) async-start(bf16[512,8,4,832]{0,3,1,2:T(8,128)(2,1)} %copy.35), calls=%async_computation.2 | async-start | bytes 54525952 | tf_op jit(solution)/shard_map/all_to_all | solution.py:50
  445.6 173.3 %all-gather.8.cloned.1.call-start = ((), (), s32[]{:S(2)}) async-start(), calls=%async_computation.11 | async-start | bytes 1310720 | tf_op jit(solution)/shard_map/all_gather | solution.py:54
  446.4 391.8 %reduce-scatter.18.cloned.1.call-start = ((), (), s32[]{:S(2)}) async-start(), calls=%async_computation.12 | async-start | bytes 7667712 | tf_op jit(solution)/shard_map/reduce_scatter | solution.py:60
  633.5 280.2 %reduce-scatter.20.cloned.1.call-start = ((), (), s32[]{:S(2)}) async-start(), calls=%async_computation.13 | async-start | bytes 7667712 | tf_op jit(solution)/shard_map/reduce_scatter | solution.py:60
  779.7 19.4 copy-start.3
  814.6 275.2 %all-gather.10.cloned.1.call-start = ((), (), s32[]{:S(2)}) async-start(), calls=%async_computation.14 | async-start | bytes 7667712 | tf_op jit(solution)/shard_map/all_gather | solution.py:66
  917.7 1.6 collective-permute-start
  919.4 8.4 collective-permute-start.1
  927.8 14.1 collective-permute-start.2
  941.9 8.3 collective-permute-start.3
  950.2 7.4 collective-permute-start.4
  1022.5 129.0 %reduce-scatter.22.cloned.1.call-start = ((), (), s32[]{:S(2)}) async-start(), calls=%async_computation.15 | async-start | bytes 2621440 | tf_op jit(solution)/shard_map/reduce_scatter | solution.py:72
  1089.8 13.6 copy-start.1
  1117.5 62.6 %all-gather.12.cloned.1.call-start = ((), (), s32[]{:S(2)}) async-start(), calls=%async_computation.16 | async-start | bytes 1310720 | tf_op jit(solution)/shard_map/all_gather | solution.py:54
  1153.2 124.3 %reduce-scatter.28.cloned.1.call-start = ((), (), s32[]{:S(2)}) async-start(), calls=%async_computation.23 | async-start | bytes 7667712 | tf_op jit(solution)/shard_map/reduce_scatter | solution.py:60
  1202.7 1.2 copy-start.4
  1202.8 150.3 %reduce-scatter.30.cloned.1.call-start = ((), (), s32[]{:S(2)}) async-start(), calls=%async_computation.24 | async-start | bytes 7667712 | tf_op jit(solution)/shard_map/reduce_scatter | solution.py:60
  1228.1 301.7 %all-gather.14.cloned.1.call-start = ((), (), s32[]{:S(2)}) async-start(), calls=%async_computation.17 | async-start | bytes 7667712 | tf_op jit(solution)/shard_map/all_gather | solution.py:66
  1357.2 1.6 collective-permute-start.5
  1358.8 8.4 collective-permute-start.6
  1367.2 14.1 collective-permute-start.7
  1381.4 8.3 collective-permute-start.8
  1389.7 7.4 collective-permute-start.9
  1462.5 128.9 %reduce-scatter.24.cloned.1.call-start = ((), (), s32[]{:S(2)}) async-start(), calls=%async_computation.18 | async-start | bytes 2621440 | tf_op jit(solution)/shard_map/reduce_scatter | solution.py:72
  1529.8 13.6 copy-start.2
  1557.5 62.8 %all-gather.16.cloned.1.call-start = ((), (), s32[]{:S(2)}) async-start(), calls=%async_computation.19 | async-start | bytes 1310720 | tf_op jit(solution)/shard_map/all_gather | solution.py:54
  1593.3 124.5 %reduce-scatter.32.cloned.1.call-start = ((), (), s32[]{:S(2)}) async-start(), calls=%async_computation.25 | async-start | bytes 7667712 | tf_op jit(solution)/shard_map/reduce_scatter | solution.py:60
  1642.9 1.2 copy-start.5
  1642.9 150.3 %reduce-scatter.34.cloned.1.call-start = ((), (), s32[]{:S(2)}) async-start(), calls=%async_computation.26 | async-start | bytes 7667712 | tf_op jit(solution)/shard_map/reduce_scatter | solution.py:60
  1668.3 301.7 %all-gather.18.cloned.1.call-start = ((), (), s32[]{:S(2)}) async-start(), calls=%async_computation.20 | async-start | bytes 7667712 | tf_op jit(solution)/shard_map/all_gather | solution.py:66
  1797.3 1.6 collective-permute-start.10
  1799.0 8.4 collective-permute-start.11
  1807.4 14.1 collective-permute-start.12
  1821.5 8.3 collective-permute-start.13
  1829.9 7.4 collective-permute-start.14
  1902.7 142.6 %all-gather.20.cloned.1.call-start = ((), (), s32[]{:S(2)}) async-start(), calls=%async_computation.22 | async-start | bytes 8519680 | tf_op jit(solution)/shard_map/all_gather | solution.py:75
  1904.1 179.3 %reduce-scatter.26.cloned.1.call-start = ((), (), s32[]{:S(2)}) async-start(), calls=%async_computation.21 | async-start | bytes 2621440 | tf_op jit(solution)/shard_map/reduce_scatter | solution.py:72
  1970.0 14.8 copy-start
Sparse Core Ops, SparseCore 0:
  448.3 170.5 all-gather.7
  633.6 204.5 reduce-scatter.17
  840.5 73.1 reduce-scatter.19
  1022.6 67.1 all-gather.9
  1117.6 33.7 reduce-scatter.21
  1153.7 26.3 all-gather.11
  1202.9 74.6 reduce-scatter.27
  1279.9 73.1 reduce-scatter.29
  1462.6 67.1 all-gather.13
  1557.6 33.7 reduce-scatter.23
  1593.9 26.3 all-gather.15
  1643.0 74.6 reduce-scatter.31
  1720.1 73.1 reduce-scatter.33
  1902.8 67.1 all-gather.17
  1972.3 72.9 all-gather.19
  2048.2 35.1 reduce-scatter.25

commit v3 on v2

--- a/solution.py
+++ b/solution.py
@@ -3,11 +3,13 @@
 import jax
 import jax.numpy as jnp
 from jax import lax
-from jax.sharding import PartitionSpec as P
+from jax.experimental.layout import Layout, with_layout_constraint
+from jax.sharding import Mesh, PartitionSpec as P
 
 FF = 53248
 POWER = 2
 HALVES = 2
+COL = ("chip", "core")
 
 
 def all_sum(value, axes):
@@ -31,7 +33,7 @@
         precision=lax.Precision.HIGHEST,
         preferred_element_type=jnp.float32,
     )
-    gram = all_sum(partial_gram, ("col", "grad"))
+    gram = all_sum(partial_gram, ("core", "chip", "grad"))
     lower_factor = jnp.linalg.cholesky(gram)
     return lax.linalg.triangular_solve(
         lower_factor, rows, left_side=False, lower=True, transpose_a=True
@@ -40,7 +42,8 @@
 
 def shards(gradient, test_matrix):
     n_grad = lax.axis_size("grad")
-    n_col = lax.axis_size("col")
+    n_chip = lax.axis_size("chip")
+    n_col = n_chip * lax.axis_size("core")
     n_rows, n_ff = gradient.shape
     piece = n_ff // (n_col * n_grad)
     half = piece // HALVES
@@ -48,7 +51,8 @@
     chunks = []
     for h in range(HALVES):
         moved = lax.all_to_all(split[:, :, :, h], "grad", split_axis=2, concat_axis=0, tiled=True)
-        chunks.append(moved.reshape(n_grad * n_rows, n_col * half))
+        chunk = moved.reshape(n_grad * n_rows, n_col * half)
+        chunks.append(with_layout_constraint(chunk, Layout((0, 1))))
 
     def sketch_of(row_piece):
         rows = lax.all_gather(row_piece, "grad", axis=0, tiled=True)
@@ -57,15 +61,17 @@
             partial = lax.dot_general(
                 chunk, rows, (((0,), (0,)), ((), ())), preferred_element_type=jnp.float32
             )
-            parts.append(lax.psum_scatter(partial, "col", scatter_dimension=0, tiled=True))
+            parts.append(lax.psum_scatter(partial, COL, scatter_dimension=0, tiled=True))
         return jnp.concatenate(parts, axis=0)
 
     sketch = sketch_of(test_matrix)
     for iteration in range(POWER + 1):
         basis_rows = orthonormal(sketch)
         basis_bf = lax.all_gather(
-            basis_rows.astype(jnp.bfloat16).reshape(HALVES, half, -1), "col", axis=1, tiled=True
+            basis_rows.astype(jnp.bfloat16).reshape(HALVES, 1, half, -1), "chip", axis=1, tiled=True
         )
+        basis_bf = lax.all_gather(basis_bf, "core", axis=1)
+        basis_bf = jnp.swapaxes(basis_bf, 1, 2).reshape(HALVES, n_col * half, -1)
         partial = jnp.dot(chunks[0], basis_bf[0], preferred_element_type=jnp.float32)
         for h in range(1, HALVES):
             partial = partial + jnp.dot(chunks[h], basis_bf[h], preferred_element_type=jnp.float32)
@@ -77,10 +83,12 @@
 
 
 def solution(mesh):
+    n_grad, n_col = mesh.devices.shape
+    split_mesh = Mesh(mesh.devices.reshape(n_grad, n_col // 2, 2), ("grad",) + COL)
     return jax.shard_map(
         shards,
-        mesh=mesh,
-        in_specs=(P(("grad", "col"), None), P(("grad", "col"), None)),
-        out_specs=(P(("grad", "col"), None), P("col", None)),
+        mesh=split_mesh,
+        in_specs=(P(("grad",) + COL, None), P(("grad",) + COL, None)),
+        out_specs=(P(("grad",) + COL, None), P(COL, None)),
         check_vma=False,
     )

time: 2100 us -> 2210 us (1.052)
  local copies, waits for them, and re-layouts: 313 us -> 413 us
    reshape x0 -> x4, local copies, waits for them, and re-layouts: none -> 178 us  [shards(): chunk = moved.reshape(n_grad * n_rows, n_col * half)]
    all_to_all x2 -> x0, local copies, waits for them, and re-layouts: 62.7 us -> none  [shards(): lax.all_to_all(split[:, :, :, h], 'grad', split_axis=2, concat_axis=0, ti...]
    all_gather x3 -> x6, waiting for transfers between devices: 199 us -> 249 us  [the longest x3 198 us: shards(): lax.all_gather(basis_rows.astype(jnp.bfloat16).reshape(HALVES, 1, half, -...]
    all_gather x3, waiting for transfers between devices: 176 us -> 137 us  [sketch_of(): rows = lax.all_gather(row_piece, 'grad', axis=0, tiled=True)]
    unnamed x24 -> x16, local copies, waits for them, and re-layouts: 157 us -> 119 us
  transfers between devices with their start and end apart: 33 -> 36, of which waited for: 33 -> 35; matrix products, arithmetic and copies ran while one was open for 11% -> 15% of each run, Pallas kernels for 0% -> 0%
where the time goes in v3:
time: 2210 us; the launch traced here: 2200 us
  waiting for transfers between devices  1360 us (62%)
  local copies, waits for them, and re-layouts  413 us (19%)
  matrix products  203 us (9%)
  other arithmetic  169 us (8%)
  starting transfers between devices  32.1 us (1%)
    all_to_all x2, waiting for transfers between devices, shards(): lax.all_to_all(split[:, :, :, h], 'grad', split_axis=2, concat_axis=0, ti...  392 us
    reduce_scatter x6, waiting for transfers between devices, sketch_of(): lax.psum_scatter(partial, COL, scatter_dimension=0, tiled=True)  335 us
    all_gather x3, waiting for transfers between devices, shards(): lax.all_gather(basis_rows.astype(jnp.bfloat16).reshape(HALVES, 1, half, -...  198 us
    reshape x4, local copies, waits for them, and re-layouts, shards(): chunk = moved.reshape(n_grad * n_rows, n_col * half)  178 us
    all_gather x3, waiting for transfers between devices, sketch_of(): rows = lax.all_gather(row_piece, 'grad', axis=0, tiled=True)  137 us
    unnamed x16, local copies, waits for them, and re-layouts  119 us
    ppermute x15, waiting for transfers between devices, all_sum(): lax.ppermute(value, axis, [(i, i ^ step) for i in range(size)])  108 us
    another operation x20, other arithmetic, orthonormal(): lower_factor = jnp.linalg.cholesky(gram)  104 us
  transfers between devices with their start and end apart: 36, of which 35 were waited for; matrix products, arithmetic and copies ran while one was open for 15% of the time, Pallas kernels for 0%

profile of v3, /device:TPU:0, one launch (start us, length us, event | category | flops | bytes accessed | tf_op | source)
XLA Modules:
  0.0 2199.4 jit_solution(16677149295387755852)
XLA Ops:
  7.2 70.6 %copy.64 = bf16[512,53248]{0,1:T(8,128)(2,1)} copy(bf16[512,53248]{1,0:T(8,128)(2,1)} %param.5) | data formatting | bytes 109051904 | tf_op args[0]
  77.8 35.6 %slice_bitcast_fusion = (bf16[512,8,4,832]{0,3,2,1:T(8,128)(2,1)}, bf16[512,8,4,832]{0,3,2,1:T(8,128)(2,1)}) fusion(bf16[512,8,4,2,832]{0,4,3,2,1:T(8,128)(2,1)} %bitcast.181), kind=kLoop, calls=%fused_computation.6 | loop fusion | bytes 109051904 | tf_op jit(solution)/shard_map/squeeze | solution.py:53
  113.4 18.7 copy.65
  132.2 8.7 all-to-all-start
  140.9 18.8 copy.68
  159.7 277.3 %all-to-all-done = bf16[512,8,4,832]{0,3,1,2:T(8,128)(2,1)} async-done(((bf16[512,8,4,832]{0,3,1,2:T(8,128)(2,1)}), bf16[512,8,4,832]{0,3,1,2:T(8,128)(2,1)}, u32[]{:S(2)}, u32[]{:S(2)}) %all-to-all-start) | async-done | bytes 27263008 | tf_op jit(solution)/shard_map/all_to_all | solution.py:53
  437.0 8.8 all-to-all-start.1
  446.6 43.2 %copy.101 = bf16[4,512,8,1,832]{4,2,1,0,3:T(8,128)(2,1)} copy(bf16[4,512,8,1,832]{1,4,2,0,3:T(8,128)(2,1)} %bitcast.3) | data formatting | bytes 54525952 | tf_op jit(solution)/shard_map/reshape | solution.py:54
  489.8 45.9 %reshape.100 = bf16[2048,6656]{1,0:T(8,128)(2,1)} reshape(bf16[4,512,8,1,832]{4,2,1,0,3:T(8,128)(2,1)} %copy.101) | data formatting | bytes 54525952 | tf_op jit(solution)/shard_map/reshape | solution.py:54
  535.6 83.5 %all-gather.14.cloned.1.call-done = bf16[2048,256]{1,0:T(8,128)(2,1)} async-done(((bf16[512,256]{1,0:T(8,128)(2,1)}), bf16[2048,256]{1,0:T(8,128)(2,1)}) %all-gather.14.cloned.1.call-update) | async-done | bytes 1048592 | tf_op jit(solution)/shard_map/all_gather | solution.py:58
  619.1 14.6 fusion.43
  633.9 114.6 %all-to-all-done.1 = bf16[512,8,4,832]{0,3,1,2:T(8,128)(2,1)} async-done(((bf16[512,8,4,832]{0,3,1,2:T(8,128)(2,1)}), bf16[512,8,4,832]{0,3,1,2:T(8,128)(2,1)}, u32[]{:S(2)}, u32[]{:S(2)}) %all-to-all-start.1) | async-done | bytes 27263008 | tf_op jit(solution)/shard_map/all_to_all | solution.py:53
  748.5 43.3 %copy.102 = bf16[4,512,8,1,832]{4,2,1,0,3:T(8,128)(2,1)} copy(bf16[4,512,8,1,832]{1,4,2,0,3:T(8,128)(2,1)} %bitcast.6) | data formatting | bytes 54525952 | tf_op jit(solution)/shard_map/reshape | solution.py:54
  791.9 46.1 %reshape.101 = bf16[2048,6656]{1,0:T(8,128)(2,1)} reshape(bf16[4,512,8,1,832]{4,2,1,0,3:T(8,128)(2,1)} %copy.102) | data formatting | bytes 54525952 | tf_op jit(solution)/shard_map/reshape | solution.py:54
  838.0 15.3 fusion.44
  854.8 88.5 %reduce-scatter.20.cloned.1.call-done = f32[832,256]{1,0:T(8,128)} async-done(((f32[6656,256]{1,0:T(8,128)}), f32[832,256]{1,0:T(8,128)}) %reduce-scatter.20.cloned.1.call-update) | async-done | bytes 851984 | tf_op jit(solution)/shard_map/reduce_scatter | solution.py:64
  949.2 8.3 collective-permute-done.1
  958.2 13.4 collective-permute-done.2
  987.6 11.7 cholesky.172
  999.4 9.8 custom-call.15
  1009.7 12.2 cholesky.189
  1027.7 19.7 custom-call.16
  1052.3 66.0 %all-gather.16.cloned.1.call-done = bf16[2,4,832,256]{3,2,0,1:T(8,128)(2,1)} async-done(((bf16[2,1,832,256]{3,2,0,1:T(8,128)(2,1)}), bf16[2,4,832,256]{3,2,0,1:T(8,128)(2,1)}) %all-gather.16.cloned.1.call-update) | async-done | bytes 3407888 | tf_op jit(solution)/shard_map/all_gather | solution.py:70
  1118.5 17.3 all-gather.28.cloned.1.call-done
  1141.9 14.5 fusion.46
  1158.3 15.8 fusion.2
  1174.3 36.5 %reduce-scatter.22.cloned.1.call-done = f32[512,256]{0,1:T(8,128)} async-done(((f32[2048,256]{0,1:T(8,128)}), f32[512,256]{0,1:T(8,128)}) %reduce-scatter.22.cloned.1.call-update) | async-done | bytes 524304 | tf_op jit(solution)/shard_map/reduce_scatter | solution.py:78
  1212.8 26.7 %all-gather.18.cloned.1.call-done = bf16[2048,256]{0,1:T(8,128)(2,1)} async-done(((bf16[512,256]{0,1:T(8,128)(2,1)}), bf16[2048,256]{0,1:T(8,128)(2,1)}) %all-gather.18.cloned.1.call-update) | async-done | bytes 1048592 | tf_op jit(solution)/shard_map/all_gather | solution.py:58
  1239.5 14.5 convolution_bitcast_fusion.3
  1254.0 8.1 copy.104
  1263.3 16.0 convolution_bitcast_fusion.2
  1279.3 8.2 copy.106
  1287.9 49.0 %reduce-scatter.28.cloned.1.call-done = f32[832,256]{1,0:T(8,128)} async-done(((f32[6656,256]{1,0:T(8,128)}), f32[832,256]{1,0:T(8,128)}) %reduce-scatter.28.cloned.1.call-update) | async-done | bytes 851984 | tf_op jit(solution)/shard_map/reduce_scatter | solution.py:64
  1338.2 74.3 %reduce-scatter.30.cloned.1.call-done = f32[832,256]{1,0:T(8,128)} async-done(((f32[6656,256]{1,0:T(8,128)}), f32[832,256]{1,0:T(8,128)}) %reduce-scatter.30.cloned.1.call-update) | async-done | bytes 851984 | tf_op jit(solution)/shard_map/reduce_scatter | solution.py:64
  1418.3 8.3 collective-permute-done.6
  1427.3 13.4 collective-permute-done.7
  1456.7 11.7 cholesky.206
  1468.5 9.8 custom-call.17
  1478.8 11.9 cholesky.223
  1497.1 19.7 custom-call.18
  1521.6 66.0 %all-gather.20.cloned.1.call-done = bf16[2,4,832,256]{3,2,0,1:T(8,128)(2,1)} async-done(((bf16[2,1,832,256]{3,2,0,1:T(8,128)(2,1)}), bf16[2,4,832,256]{3,2,0,1:T(8,128)(2,1)}) %all-gather.20.cloned.1.call-update) | async-done | bytes 3407888 | tf_op jit(solution)/shard_map/all_gather | solution.py:70
  1587.9 17.4 all-gather.30.cloned.1.call-done
  1611.4 14.5 fusion.48
  1627.9 15.8 fusion.1
  1643.8 36.5 %reduce-scatter.24.cloned.1.call-done = f32[512,256]{0,1:T(8,128)} async-done(((f32[2048,256]{0,1:T(8,128)}), f32[512,256]{0,1:T(8,128)}) %reduce-scatter.24.cloned.1.call-update) | async-done | bytes 524304 | tf_op jit(solution)/shard_map/reduce_scatter | solution.py:78
  1682.5 26.6 %all-gather.22.cloned.1.call-done = bf16[2048,256]{0,1:T(8,128)(2,1)} async-done(((bf16[512,256]{0,1:T(8,128)(2,1)}), bf16[2048,256]{0,1:T(8,128)(2,1)}) %all-gather.22.cloned.1.call-update) | async-done | bytes 1048592 | tf_op jit(solution)/shard_map/all_gather | solution.py:58
  1709.1 14.5 convolution_bitcast_fusion.1
  1723.5 8.1 copy.108
  1732.9 16.0 convolution_bitcast_fusion
  1748.8 8.2 copy.110
  1757.2 49.3 %reduce-scatter.32.cloned.1.call-done = f32[832,256]{1,0:T(8,128)} async-done(((f32[6656,256]{1,0:T(8,128)}), f32[832,256]{1,0:T(8,128)}) %reduce-scatter.32.cloned.1.call-update) | async-done | bytes 851984 | tf_op jit(solution)/shard_map/reduce_scatter | solution.py:64
  1807.7 74.1 %reduce-scatter.34.cloned.1.call-done = f32[832,256]{1,0:T(8,128)} async-done(((f32[6656,256]{1,0:T(8,128)}), f32[832,256]{1,0:T(8,128)}) %reduce-scatter.34.cloned.1.call-update) | async-done | bytes 851984 | tf_op jit(solution)/shard_map/reduce_scatter | solution.py:64
  1887.6 8.3 collective-permute-done.11
  1896.6 13.4 collective-permute-done.12
  1926.1 11.7 cholesky.240
  1937.9 9.8 custom-call.19
  1948.2 11.9 cholesky.257
  1966.8 19.7 custom-call.20
  1991.3 66.0 %all-gather.24.cloned.1.call-done = bf16[2,4,832,256]{3,2,0,1:T(8,128)(2,1)} async-done(((bf16[2,1,832,256]{3,2,0,1:T(8,128)(2,1)}), bf16[2,4,832,256]{3,2,0,1:T(8,128)(2,1)}) %all-gather.24.cloned.1.call-update) | async-done | bytes 3407888 | tf_op jit(solution)/shard_map/all_gather | solution.py:70
  2059.1 15.8 all-gather.32.cloned.1.call-done
  2081.1 15.6 fusion.50
  2096.7 15.8 fusion
  2112.6 39.6 %all-gather.26.cloned.1.call-done = f32[6656,256]{0,1:T(8,128)} async-done(((f32[1664,256]{0,1:T(8,128)}), f32[6656,256]{0,1:T(8,128)}) %all-gather.26.cloned.1.call-update) | async-done | bytes 6815760 | tf_op jit(solution)/shard_map/all_gather | solution.py:81
  2160.3 30.1 %reduce-scatter.26.cloned.1.call-done = f32[512,256]{0,1:T(8,128)} async-done(((f32[2048,256]{0,1:T(8,128)}), f32[512,256]{0,1:T(8,128)}) %reduce-scatter.26.cloned.1.call-update) | async-done | bytes 524304 | tf_op jit(solution)/shard_map/reduce_scatter | solution.py:78
  (183 shorter events, 157.1 us)
Async XLA Ops:
  132.2 304.9 %all-to-all-start = ((bf16[512,8,4,832]{0,3,1,2:T(8,128)(2,1)}), bf16[512,8,4,832]{0,3,1,2:T(8,128)(2,1)}, u32[]{:S(2)}, u32[]{:S(2)}) async-start(bf16[512,8,4,832]{0,3,1,2:T(8,128)(2,1)} %copy.65), calls=%async_computation | async-start | bytes 54525952 | tf_op jit(solution)/shard_map/all_to_all | solution.py:53
  437.0 311.5 %all-to-all-start.1 = ((bf16[512,8,4,832]{0,3,1,2:T(8,128)(2,1)}), bf16[512,8,4,832]{0,3,1,2:T(8,128)(2,1)}, u32[]{:S(2)}, u32[]{:S(2)}) async-start(bf16[512,8,4,832]{0,3,1,2:T(8,128)(2,1)} %copy.68), calls=%async_computation.2 | async-start | bytes 54525952 | tf_op jit(solution)/shard_map/all_to_all | solution.py:53
  445.8 173.3 %all-gather.14.cloned.1.call-start = ((), (), s32[]{:S(2)}) async-start(), calls=%async_computation.11 | async-start | bytes 1310720 | tf_op jit(solution)/shard_map/all_gather | solution.py:58
  446.6 407.1 %reduce-scatter.18.cloned.1.call-start = ((), (), s32[]{:S(2)}) async-start(), calls=%async_computation.12 | async-start | bytes 7667712 | tf_op jit(solution)/shard_map/reduce_scatter | solution.py:64
  633.7 309.7 %reduce-scatter.20.cloned.1.call-start = ((), (), s32[]{:S(2)}) async-start(), calls=%async_computation.13 | async-start | bytes 7667712 | tf_op jit(solution)/shard_map/reduce_scatter | solution.py:64
  791.9 46.1 %copy-start = (bf16[2048,256]{1,0:T(8,128)(2,1)S(1)}, bf16[2048,256]{1,0:T(8,128)(2,1)}, u32[]{:S(2)}) copy-start(bf16[2048,256]{1,0:T(8,128)(2,1)} %all-gather.14.cloned.1.call-done) | copy-start | bytes 3145732
  853.3 265.0 %all-gather.16.cloned.1.call-start = ((), (), s32[]{:S(2)}) async-start(), calls=%async_computation.14 | async-start | bytes 4259840 | tf_op jit(solution)/shard_map/all_gather | solution.py:70
  947.4 1.6 collective-permute-start
  949.1 8.4 collective-permute-start.1
  957.5 14.1 collective-permute-start.2
  971.6 8.3 collective-permute-start.3
  980.0 7.4 collective-permute-start.4
  1052.2 83.6 %all-gather.28.cloned.1.call-start = ((), (), s32[]{:S(2)}) async-start(), calls=%async_computation.23 | async-start | bytes 10223616 | tf_op jit(solution)/shard_map/all_gather | solution.py:73
  1118.3 92.4 %reduce-scatter.22.cloned.1.call-start = ((), (), s32[]{:S(2)}) async-start(), calls=%async_computation.15 | async-start | bytes 2621440 | tf_op jit(solution)/shard_map/reduce_scatter | solution.py:78
  1174.2 65.3 %all-gather.18.cloned.1.call-start = ((), (), s32[]{:S(2)}) async-start(), calls=%async_computation.16 | async-start | bytes 1310720 | tf_op jit(solution)/shard_map/all_gather | solution.py:58
  1212.5 124.4 %reduce-scatter.28.cloned.1.call-start = ((), (), s32[]{:S(2)}) async-start(), calls=%async_computation.26 | async-start | bytes 7667712 | tf_op jit(solution)/shard_map/reduce_scatter | solution.py:64
  1262.1 1.2 copy-start.1
  1262.1 150.3 %reduce-scatter.30.cloned.1.call-start = ((), (), s32[]{:S(2)}) async-start(), calls=%async_computation.27 | async-start | bytes 7667712 | tf_op jit(solution)/shard_map/reduce_scatter | solution.py:64
  1287.5 300.2 %all-gather.20.cloned.1.call-start = ((), (), s32[]{:S(2)}) async-start(), calls=%async_computation.17 | async-start | bytes 4259840 | tf_op jit(solution)/shard_map/all_gather | solution.py:70
  1416.5 1.6 collective-permute-start.5
  1418.2 8.4 collective-permute-start.6
  1426.6 14.1 collective-permute-start.7
  1440.7 8.3 collective-permute-start.8
  1449.1 7.4 collective-permute-start.9
  1521.6 83.8 %all-gather.30.cloned.1.call-start = ((), (), s32[]{:S(2)}) async-start(), calls=%async_computation.24 | async-start | bytes 10223616 | tf_op jit(solution)/shard_map/all_gather | solution.py:73
  1587.7 92.6 %reduce-scatter.24.cloned.1.call-start = ((), (), s32[]{:S(2)}) async-start(), calls=%async_computation.18 | async-start | bytes 2621440 | tf_op jit(solution)/shard_map/reduce_scatter | solution.py:78
  1643.7 65.3 %all-gather.22.cloned.1.call-start = ((), (), s32[]{:S(2)}) async-start(), calls=%async_computation.19 | async-start | bytes 1310720 | tf_op jit(solution)/shard_map/all_gather | solution.py:58
  1682.1 124.4 %reduce-scatter.32.cloned.1.call-start = ((), (), s32[]{:S(2)}) async-start(), calls=%async_computation.28 | async-start | bytes 7667712 | tf_op jit(solution)/shard_map/reduce_scatter | solution.py:64
  1731.6 1.2 copy-start.2
  1731.7 150.2 %reduce-scatter.34.cloned.1.call-start = ((), (), s32[]{:S(2)}) async-start(), calls=%async_computation.29 | async-start | bytes 7667712 | tf_op jit(solution)/shard_map/reduce_scatter | solution.py:64
  1757.0 300.3 %all-gather.24.cloned.1.call-start = ((), (), s32[]{:S(2)}) async-start(), calls=%async_computation.20 | async-start | bytes 4259840 | tf_op jit(solution)/shard_map/all_gather | solution.py:70
  1885.9 1.6 collective-permute-start.10
  1887.6 8.4 collective-permute-start.11
  1896.0 14.1 collective-permute-start.12
  1910.1 8.3 collective-permute-start.13
  1918.4 7.4 collective-permute-start.14
  1991.3 83.6 %all-gather.32.cloned.1.call-start = ((), (), s32[]{:S(2)}) async-start(), calls=%async_computation.25 | async-start | bytes 10223616 | tf_op jit(solution)/shard_map/all_gather | solution.py:73
  2057.3 94.8 %all-gather.26.cloned.1.call-start = ((), (), s32[]{:S(2)}) async-start(), calls=%async_computation.22 | async-start | bytes 8519680 | tf_op jit(solution)/shard_map/all_gather | solution.py:81
  2058.8 131.6 %reduce-scatter.26.cloned.1.call-start = ((), (), s32[]{:S(2)}) async-start(), calls=%async_computation.21 | async-start | bytes 2621440 | tf_op jit(solution)/shard_map/reduce_scatter | solution.py:78
Sparse Core Ops, SparseCore 0:
  448.5 170.5 all-gather.13
  633.8 204.5 reduce-scatter.17
  853.4 89.8 reduce-scatter.19
  1052.3 65.8 all-gather.15
  1119.7 16.1 all-gather.27
  1174.3 36.3 reduce-scatter.21
  1213.1 26.3 all-gather.17
  1262.2 74.6 reduce-scatter.27
  1339.3 73.1 reduce-scatter.29
  1521.7 65.9 all-gather.19
  1589.2 16.1 all-gather.29
  1643.9 36.3 reduce-scatter.23
  1682.6 26.3 all-gather.21
  1731.8 74.6 reduce-scatter.31
  1808.6 73.1 reduce-scatter.33
  1991.4 65.8 all-gather.23
  2058.7 16.1 all-gather.31
  2076.6 75.5 all-gather.25
  2155.1 35.1 reduce-scatter.25

commit v4 on v2

--- a/solution.py
+++ b/solution.py
@@ -21,6 +21,28 @@
             value = value + lax.ppermute(value, axis, [(i, i ^ step) for i in range(size)])
             step *= 2
     return value
+
+
+def grad_gather(value):
+    size = lax.axis_size("grad")
+    index = lax.axis_index("grad")
+    received = [value] + [
+        lax.ppermute(value, "grad", [(i, (i + s) % size) for i in range(size)])
+        for s in range(1, size)
+    ]
+    ordered = jnp.roll(jnp.stack(received)[::-1], index + 1, axis=0)
+    return ordered.reshape((size * value.shape[0],) + value.shape[1:])
+
+
+def grad_scatter_sum(value):
+    size = lax.axis_size("grad")
+    index = lax.axis_index("grad")
+    pieces = value.reshape((size, value.shape[0] // size) + value.shape[1:])
+    total = lax.dynamic_index_in_dim(pieces, index, keepdims=False)
+    for s in range(1, size):
+        outgoing = lax.dynamic_index_in_dim(pieces, (index + s) % size, keepdims=False)
+        total = total + lax.ppermute(outgoing, "grad", [(i, (i + s) % size) for i in range(size)])
+    return total
 
 
 def orthonormal(rows):
@@ -51,7 +73,7 @@
         chunks.append(moved.reshape(n_grad * n_rows, n_col * half))
 
     def sketch_of(row_piece):
-        rows = lax.all_gather(row_piece, "grad", axis=0, tiled=True)
+        rows = grad_gather(row_piece)
         parts = []
         for chunk in chunks:
             partial = lax.dot_general(
@@ -69,10 +91,10 @@
         partial = jnp.dot(chunks[0], basis_bf[0], preferred_element_type=jnp.float32)
         for h in range(1, HALVES):
             partial = partial + jnp.dot(chunks[h], basis_bf[h], preferred_element_type=jnp.float32)
-        reduced = lax.psum_scatter(partial, "grad", scatter_dimension=0, tiled=True)
+        reduced = grad_scatter_sum(partial)
         if iteration < POWER:
             sketch = sketch_of(reduced.astype(jnp.bfloat16))
-    projector = lax.all_gather(basis_rows * math.sqrt(FF), "grad", axis=0, tiled=True)
+    projector = grad_gather(basis_rows * math.sqrt(FF))
     return (reduced, projector)
 
 

time: 2100 us -> 2090 us (level)
  waiting for transfers between devices: 1360 us -> 1270 us
  local copies, waits for them, and re-layouts: 313 us -> 365 us
  starting transfers between devices: 31.8 us -> 55.1 us
    ppermute x0 -> x21, waiting for transfers between devices: none -> 371 us  [the longest x12 325 us: grad_gather(): lax.ppermute(value, 'grad', [(i, (i + s) % size) for i in range(size)])]
    all_gather x4 -> x0, waiting for transfers between devices: 222 us -> none  [the longest x3 176 us: sketch_of(): rows = lax.all_gather(row_piece, 'grad', axis=0, tiled=True)]
    all_to_all x2, waiting for transfers between devices: 392 us -> 277 us  [shards(): lax.all_to_all(split[:, :, :, h], 'grad', split_axis=2, concat_axis=0, ti...]
    reduce_scatter x3 -> x0, waiting for transfers between devices: 97.7 us -> none  [shards(): reduced = lax.psum_scatter(partial, 'grad', scatter_dimension=0, tiled=True)]
    dynamic_slice x0 -> x16, local copies, waits for them, and re-layouts: none -> 34.4 us  [the longest x6 19.5 us: grad_scatter_sum(): total = lax.dynamic_index_in_dim(pieces, index, keepdims=False)]
    reduce_scatter x6, waiting for transfers between devices: 345 us -> 316 us  [sketch_of(): lax.psum_scatter(partial, 'col', scatter_dimension=0, tiled=True)]
    ppermute x0 -> x21, starting transfers between devices: none -> 24.4 us  [the longest x12 13.5 us: grad_gather(): lax.ppermute(value, 'grad', [(i, (i + s) % size) for i in range(size)])]
    unnamed x24 -> x22, local copies, waits for them, and re-layouts: 157 us -> 161 us
  transfers between devices with their start and end apart: 33 -> 47, of which waited for: 33 -> 34; matrix products, arithmetic and copies ran while one was open for 11% -> 14% of each run, Pallas kernels for 0% -> 0%
where the time goes in v4:
time: 2090 us; the launch traced here: 2080 us
  waiting for transfers between devices  1270 us (61%)
  local copies, waits for them, and re-layouts  365 us (17%)
  matrix products  193 us (9%)
  other arithmetic  184 us (9%)
  starting transfers between devices  55.1 us (3%)
    ppermute x12, waiting for transfers between devices, grad_gather(): lax.ppermute(value, 'grad', [(i, (i + s) % size) for i in range(size)])  325 us
    reduce_scatter x6, waiting for transfers between devices, sketch_of(): lax.psum_scatter(partial, 'col', scatter_dimension=0, tiled=True)  316 us
    all_to_all x2, waiting for transfers between devices, shards(): lax.all_to_all(split[:, :, :, h], 'grad', split_axis=2, concat_axis=0, ti...  277 us
    all_gather x3, waiting for transfers between devices, shards(): lax.all_gather(basis_rows.astype(jnp.bfloat16).reshape(HALVES, half, -1),...  196 us
    unnamed x22, local copies, waits for them, and re-layouts  161 us
    ppermute x15, waiting for transfers between devices, all_sum(): lax.ppermute(value, axis, [(i, i ^ step) for i in range(size)])  108 us
    another operation x20, other arithmetic, orthonormal(): lower_factor = jnp.linalg.cholesky(gram)  104 us
    dot_general x6, matrix products, sketch_of(): lax.dot_general(chunk, rows, (((0,), (0,)), ((), ())), preferred_element_...  94 us
  transfers between devices with their start and end apart: 47, of which 34 were waited for; matrix products, arithmetic and copies ran while one was open for 14% of the time, Pallas kernels for 0%

profile of v4, /device:TPU:0, one launch (start us, length us, event | category | flops | bytes accessed | tf_op | source)
XLA Modules:
  0.0 2082.9 jit_solution(17427826224156796190)
XLA Ops:
  7.2 70.6 %copy.45 = bf16[512,53248]{0,1:T(8,128)(2,1)} copy(bf16[512,53248]{1,0:T(8,128)(2,1)} %param.7) | data formatting | bytes 109051904 | tf_op args[0]
  77.8 35.5 %slice_bitcast_fusion.1 = (bf16[512,8,4,832]{0,3,2,1:T(8,128)(2,1)}, bf16[512,8,4,832]{0,3,2,1:T(8,128)(2,1)}) fusion(bf16[512,8,4,2,832]{0,4,3,2,1:T(8,128)(2,1)} %bitcast.268), kind=kLoop, calls=%fused_computation.7 | loop fusion | bytes 109051904 | tf_op jit(solution)/shard_map/squeeze | solution.py:72
  113.3 18.7 copy.46
  132.0 8.7 all-to-all-start
  140.7 19.2 copy.48
  159.9 276.9 %all-to-all-done = bf16[512,8,4,832]{0,3,1,2:T(8,128)(2,1)} async-done(((bf16[512,8,4,832]{0,3,1,2:T(8,128)(2,1)}), bf16[512,8,4,832]{0,3,1,2:T(8,128)(2,1)}, u32[]{:S(2)}, u32[]{:S(2)}) %all-to-all-start) | async-done | bytes 27263008 | tf_op jit(solution)/shard_map/all_to_all | solution.py:72
  436.9 8.7 all-to-all-start.1
  449.6 297.4 %collective-permute-done.2 = bf16[512,256]{1,0:T(8,128)(2,1)S(1)} collective-permute-done((bf16[512,256]{1,0:T(8,128)(2,1)S(1)}, bf16[512,256]{1,0:T(8,128)(2,1)S(1)}, u32[]{:S(2)}, u32[]{:S(2)}) %collective-permute-start.2) | collective-permute-done | bytes 262176 | tf_op jit(solution)/shard_map/ppermute | solution.py:30
  752.5 31.4 %copy.47 = bf16[4,512,8,1,832]{1,0,4,2,3:T(4,128)(2,1)} copy(bf16[4,512,8,1,832]{1,4,2,0,3:T(8,128)(2,1)} %bitcast.8) | data formatting | bytes 54525952 | tf_op jit(solution)/shard_map/all_to_all | solution.py:72
  783.9 18.9 copy.96
  802.9 15.4 convolution_bitcast_fusion.5
  818.3 8.1 copy.84
  826.6 31.4 %copy.49 = bf16[4,512,8,1,832]{1,0,4,2,3:T(4,128)(2,1)} copy(bf16[4,512,8,1,832]{1,4,2,0,3:T(8,128)(2,1)} %bitcast.12) | data formatting | bytes 54525952 | tf_op jit(solution)/shard_map/all_to_all | solution.py:72
  858.0 19.2 copy.97
  877.2 15.7 convolution_bitcast_fusion.4
  892.9 8.1 copy.86
  902.6 73.5 %reduce-scatter.21.cloned.1.call-done = f32[832,256]{1,0:T(8,128)} async-done(((f32[6656,256]{1,0:T(8,128)}), f32[832,256]{1,0:T(8,128)}) %reduce-scatter.21.cloned.1.call-update) | async-done | bytes 851984 | tf_op jit(solution)/shard_map/reduce_scatter | solution.py:82
  981.8 8.3 collective-permute-done.4
  990.8 13.4 collective-permute-done.5
  1005.8 6.7 collective-permute-done.6
  1020.3 11.7 cholesky.172
  1032.1 9.8 custom-call.15
  1042.4 12.1 cholesky.189
  1060.8 19.7 custom-call.16
  1085.6 67.1 %all-gather.4.cloned.1.call-done = bf16[2,6656,256]{2,1,0:T(8,128)(2,1)} async-done(((bf16[2,832,256]{2,1,0:T(8,128)(2,1)}), bf16[2,6656,256]{2,1,0:T(8,128)(2,1)}) %all-gather.4.cloned.1.call-update) | async-done | bytes 6815760 | tf_op jit(solution)/shard_map/all_gather | solution.py:88
  1152.6 13.6 fusion.5
  1166.2 12.5 fusion.8
  1192.6 9.7 collective-permute-done.10
  1202.3 13.3 collective-permute-done.9
  1231.6 15.4 convolution_bitcast_fusion.3
  1247.0 8.1 copy.88
  1255.1 16.0 convolution_bitcast_fusion.2
  1271.2 8.2 copy.90
  1279.9 46.9 %reduce-scatter.23.cloned.1.call-done = f32[832,256]{1,0:T(8,128)} async-done(((f32[6656,256]{1,0:T(8,128)}), f32[832,256]{1,0:T(8,128)}) %reduce-scatter.23.cloned.1.call-update) | async-done | bytes 851984 | tf_op jit(solution)/shard_map/reduce_scatter | solution.py:82
  1328.0 74.1 %reduce-scatter.25.cloned.1.call-done = f32[832,256]{1,0:T(8,128)} async-done(((f32[6656,256]{1,0:T(8,128)}), f32[832,256]{1,0:T(8,128)}) %reduce-scatter.25.cloned.1.call-update) | async-done | bytes 851984 | tf_op jit(solution)/shard_map/reduce_scatter | solution.py:82
  1407.9 8.3 collective-permute-done.15
  1416.9 13.4 collective-permute-done.16
  1431.9 6.8 collective-permute-done.17
  1446.3 11.7 cholesky.206
  1458.1 9.8 custom-call.17
  1468.4 11.9 cholesky.223
  1487.2 19.7 custom-call.18
  1512.0 67.1 %all-gather.6.cloned.1.call-done = bf16[2,6656,256]{2,1,0:T(8,128)(2,1)} async-done(((bf16[2,832,256]{2,1,0:T(8,128)(2,1)}), bf16[2,6656,256]{2,1,0:T(8,128)(2,1)}) %all-gather.6.cloned.1.call-update) | async-done | bytes 6815760 | tf_op jit(solution)/shard_map/all_gather | solution.py:88
  1579.1 13.6 fusion.3
  1592.7 12.5 fusion.10
  1619.0 9.7 collective-permute-done.21
  1628.7 13.3 collective-permute-done.20
  1658.0 15.4 convolution_bitcast_fusion.1
  1673.4 8.1 copy.92
  1681.6 16.0 convolution_bitcast_fusion
  1697.6 8.2 copy.94
  1706.1 47.1 %reduce-scatter.27.cloned.1.call-done = f32[832,256]{1,0:T(8,128)} async-done(((f32[6656,256]{1,0:T(8,128)}), f32[832,256]{1,0:T(8,128)}) %reduce-scatter.27.cloned.1.call-update) | async-done | bytes 851984 | tf_op jit(solution)/shard_map/reduce_scatter | solution.py:82
  1754.4 74.3 %reduce-scatter.29.cloned.1.call-done = f32[832,256]{1,0:T(8,128)} async-done(((f32[6656,256]{1,0:T(8,128)}), f32[832,256]{1,0:T(8,128)}) %reduce-scatter.29.cloned.1.call-update) | async-done | bytes 851984 | tf_op jit(solution)/shard_map/reduce_scatter | solution.py:82
  1834.5 8.3 collective-permute-done.26
  1843.5 13.4 collective-permute-done.27
  1858.5 6.8 collective-permute-done.28
  1872.9 11.7 cholesky.240
  1884.7 9.8 custom-call.19
  1895.0 11.9 cholesky.257
  1913.6 19.7 custom-call.20
  1943.8 61.6 %all-gather.8.cloned.1.call-done = bf16[2,6656,256]{2,1,0:T(8,128)(2,1)} async-done(((bf16[2,832,256]{2,1,0:T(8,128)(2,1)}), bf16[2,6656,256]{2,1,0:T(8,128)(2,1)}) %all-gather.8.cloned.1.call-update) | async-done | bytes 6815760 | tf_op jit(solution)/shard_map/all_gather | solution.py:88
  2005.4 13.6 fusion.1
  2019.0 12.5 fusion.12
  2065.8 7.6 copy.80
  (219 shorter events, 208.0 us)
Async XLA Ops:
  132.0 304.9 %all-to-all-start = ((bf16[512,8,4,832]{0,3,1,2:T(8,128)(2,1)}), bf16[512,8,4,832]{0,3,1,2:T(8,128)(2,1)}, u32[]{:S(2)}, u32[]{:S(2)}) async-start(bf16[512,8,4,832]{0,3,1,2:T(8,128)(2,1)} %copy.46), calls=%async_computation | async-start | bytes 54525952 | tf_op jit(solution)/shard_map/all_to_all | solution.py:72
  159.9 285.7 %copy-start.4 = (bf16[512,256]{1,0:T(8,128)(2,1)S(1)}, bf16[512,256]{1,0:T(8,128)(2,1)}, u32[]{:S(2)}) copy-start(bf16[512,256]{1,0:T(8,128)(2,1)} %param.8) | copy-start | bytes 786436
  436.9 389.7 %all-to-all-start.1 = ((bf16[512,8,4,832]{0,3,1,2:T(8,128)(2,1)}), bf16[512,8,4,832]{0,3,1,2:T(8,128)(2,1)}, u32[]{:S(2)}, u32[]{:S(2)}) async-start(bf16[512,8,4,832]{0,3,1,2:T(8,128)(2,1)} %copy.48), calls=%async_computation.1 | async-start | bytes 54525952 | tf_op jit(solution)/shard_map/all_to_all | solution.py:72
  445.6 455.7 %reduce-scatter.19.cloned.1.call-start = ((), (), s32[]{:S(2)}) async-start(), calls=%async_computation.11 | async-start | bytes 7667712 | tf_op jit(solution)/shard_map/reduce_scatter | solution.py:82
  445.7 301.4 %collective-permute-start.2 = (bf16[512,256]{1,0:T(8,128)(2,1)S(1)}, bf16[512,256]{1,0:T(8,128)(2,1)S(1)}, u32[]{:S(2)}, u32[]{:S(2)}) collective-permute-start(bf16[512,256]{1,0:T(8,128)(2,1)S(1)} %copy-done.4), channel_id=1, source_target_pairs={{0,24},{8,0},{16,8},{24,16},{1,25},{9,1},{17,9},{25,17},{2,26},{10... | collective-permute-start | bytes 786440 | tf_op jit(solution)/shard_map/ppermute | solution.py:30
  448.5 298.6 %collective-permute-start.1 = (bf16[512,256]{1,0:T(8,128)(2,1)S(1)}, bf16[512,256]{1,0:T(8,128)(2,1)S(1)}, u32[]{:S(2)}, u32[]{:S(2)}) collective-permute-start(bf16[512,256]{1,0:T(8,128)(2,1)S(1)} %copy-done.4), channel_id=1, source_target_pairs={{0,16},{8,24},{16,0},{24,8},{1,17},{9,25},{17,1},{25,9},{2,18},{10... | collective-permute-start | bytes 786440 | tf_op jit(solution)/shard_map/ppermute | solution.py:30
  449.0 302.9 %collective-permute-start = (bf16[512,256]{1,0:T(8,128)(2,1)S(1)}, bf16[512,256]{1,0:T(8,128)(2,1)S(1)}, u32[]{:S(2)}, u32[]{:S(2)}) collective-permute-start(bf16[512,256]{1,0:T(8,128)(2,1)S(1)} %copy-done.4), channel_id=1, source_target_pairs={{0,8},{8,16},{16,24},{24,0},{1,9},{9,17},{17,25},{25,1},{2,10},{10... | collective-permute-start | bytes 786440 | tf_op jit(solution)/shard_map/ppermute | solution.py:30
  826.4 149.7 %reduce-scatter.21.cloned.1.call-start = ((), (), s32[]{:S(2)}) async-start(), calls=%async_computation.12 | async-start | bytes 7667712 | tf_op jit(solution)/shard_map/reduce_scatter | solution.py:82
  901.1 251.6 %all-gather.4.cloned.1.call-start = ((), (), s32[]{:S(2)}) async-start(), calls=%async_computation.8 | async-start | bytes 7667712 | tf_op jit(solution)/shard_map/all_gather | solution.py:88
  980.1 1.6 collective-permute-start.3
  981.7 8.4 collective-permute-start.4
  990.2 14.1 collective-permute-start.5
  1004.3 8.3 collective-permute-start.6
  1012.6 7.4 collective-permute-start.7
  1085.3 241.5 %reduce-scatter.23.cloned.1.call-start = ((), (), s32[]{:S(2)}) async-start(), calls=%async_computation.13 | async-start | bytes 7667712 | tf_op jit(solution)/shard_map/reduce_scatter | solution.py:82
  1152.6 13.6 copy-start
  1187.4 14.9 collective-permute-start.10
  1190.3 25.2 %collective-permute-start.9 = (f32[512,256]{1,0:T(8,128)S(1)}, f32[512,256]{1,0:T(8,128)}, u32[]{:S(2)}, u32[]{:S(2)}) collective-permute-start(f32[512,256]{1,0:T(8,128)S(1)} %bitcast.292), channel_id=1, source_target_pairs={{0,16},{8,24},{16,0},{24,8},{1,17},{9,25},{17,1},{25,9},{2,18},{10... | collective-permute-start | bytes 1572872 | tf_op jit(solution)/shard_map/ppermute | solution.py:44
  1191.5 24.1 %collective-permute-start.8 = (f32[512,256]{1,0:T(8,128)S(1)}, f32[512,256]{1,0:T(8,128)}, u32[]{:S(2)}, u32[]{:S(2)}) collective-permute-start(f32[512,256]{1,0:T(8,128)S(1)} %bitcast.294), channel_id=1, source_target_pairs={{0,8},{8,16},{16,24},{24,0},{1,9},{9,17},{17,25},{25,1},{2,10},{10... | collective-permute-start | bytes 1572872 | tf_op jit(solution)/shard_map/ppermute | solution.py:44
  1216.9 9.2 collective-permute-start.13
  1217.5 13.5 collective-permute-start.12
  1218.1 12.8 collective-permute-start.11
  1255.1 147.0 %reduce-scatter.25.cloned.1.call-start = ((), (), s32[]{:S(2)}) async-start(), calls=%async_computation.14 | async-start | bytes 7667712 | tf_op jit(solution)/shard_map/reduce_scatter | solution.py:82
  1279.4 299.7 %all-gather.6.cloned.1.call-start = ((), (), s32[]{:S(2)}) async-start(), calls=%async_computation.9 | async-start | bytes 7667712 | tf_op jit(solution)/shard_map/all_gather | solution.py:88
  1406.2 1.6 collective-permute-start.14
  1407.8 8.4 collective-permute-start.15
  1416.2 14.1 collective-permute-start.16
  1430.4 8.3 collective-permute-start.17
  1438.7 7.4 collective-permute-start.18
  1511.7 241.5 %reduce-scatter.27.cloned.1.call-start = ((), (), s32[]{:S(2)}) async-start(), calls=%async_computation.15 | async-start | bytes 7667712 | tf_op jit(solution)/shard_map/reduce_scatter | solution.py:82
  1579.1 13.6 copy-start.2
  1613.9 14.8 collective-permute-start.21
  1616.8 25.2 %collective-permute-start.20 = (f32[512,256]{1,0:T(8,128)S(1)}, f32[512,256]{1,0:T(8,128)}, u32[]{:S(2)}, u32[]{:S(2)}) collective-permute-start(f32[512,256]{1,0:T(8,128)S(1)} %bitcast.293), channel_id=1, source_target_pairs={{0,16},{8,24},{16,0},{24,8},{1,17},{9,25},{17,1},{25,9},{2,18},{10... | collective-permute-start | bytes 1572872 | tf_op jit(solution)/shard_map/ppermute | solution.py:44
  1617.9 24.1 %collective-permute-start.19 = (f32[512,256]{1,0:T(8,128)S(1)}, f32[512,256]{1,0:T(8,128)}, u32[]{:S(2)}, u32[]{:S(2)}) collective-permute-start(f32[512,256]{1,0:T(8,128)S(1)} %bitcast.295), channel_id=1, source_target_pairs={{0,8},{8,16},{16,24},{24,0},{1,9},{9,17},{17,25},{25,1},{2,10},{10... | collective-permute-start | bytes 1572872 | tf_op jit(solution)/shard_map/ppermute | solution.py:44
  1643.3 9.2 collective-permute-start.24
  1643.9 13.5 collective-permute-start.23
  1644.6 12.8 collective-permute-start.22
  1681.5 147.1 %reduce-scatter.29.cloned.1.call-start = ((), (), s32[]{:S(2)}) async-start(), calls=%async_computation.16 | async-start | bytes 7667712 | tf_op jit(solution)/shard_map/reduce_scatter | solution.py:82
  1705.8 299.6 %all-gather.8.cloned.1.call-start = ((), (), s32[]{:S(2)}) async-start(), calls=%async_computation.10 | async-start | bytes 7667712 | tf_op jit(solution)/shard_map/all_gather | solution.py:88
  1832.7 1.6 collective-permute-start.25
  1834.4 8.4 collective-permute-start.26
  1842.8 14.1 collective-permute-start.27
  1856.9 8.3 collective-permute-start.28
  1865.3 7.4 collective-permute-start.29
  1940.1 107.6 %collective-permute-start.35 = (f32[1664,256]{0,1:T(8,128)}, f32[1664,256]{0,1:T(8,128)}, u32[]{:S(2)}, u32[]{:S(2)}) collective-permute-start(f32[1664,256]{0,1:T(8,128)} %get-tuple-element.73), channel_id=1, source_target_pairs={{0,24},{8,0},{16,8},{24,16},{1,25},{9,1},{17,9},{25,17},{2,26},{10... | collective-permute-start | bytes 5111816 | tf_op jit(solution)/shard_map/ppermute | solution.py:30
  1942.5 105.8 %collective-permute-start.34 = (f32[1664,256]{0,1:T(8,128)}, f32[1664,256]{0,1:T(8,128)}, u32[]{:S(2)}, u32[]{:S(2)}) collective-permute-start(f32[1664,256]{0,1:T(8,128)} %get-tuple-element.73), channel_id=1, source_target_pairs={{0,16},{8,24},{16,0},{24,8},{1,17},{9,25},{17,1},{25,9},{2,18},{10... | collective-permute-start | bytes 5111816 | tf_op jit(solution)/shard_map/ppermute | solution.py:30
  1943.0 105.3 %collective-permute-start.33 = (f32[1664,256]{0,1:T(8,128)}, f32[1664,256]{0,1:T(8,128)}, u32[]{:S(2)}, u32[]{:S(2)}) collective-permute-start(f32[1664,256]{0,1:T(8,128)} %get-tuple-element.73), channel_id=1, source_target_pairs={{0,8},{8,16},{16,24},{24,0},{1,9},{9,17},{17,25},{25,1},{2,10},{10... | collective-permute-start | bytes 5111816 | tf_op jit(solution)/shard_map/ppermute | solution.py:30
  2005.4 13.6 copy-start.1
  2033.9 14.4 copy-start.3
  2042.4 31.5 %collective-permute-start.32 = (f32[512,256]{1,0:T(8,128)}, f32[512,256]{1,0:T(8,128)}, u32[]{:S(2)}, u32[]{:S(2)}) collective-permute-start(f32[512,256]{1,0:T(8,128)} %bitcast.287), channel_id=1, source_target_pairs={{0,24},{8,0},{16,8},{24,16},{1,25},{9,1},{17,9},{25,17},{2,26},{10... | collective-permute-start | bytes 1572872 | tf_op jit(solution)/shard_map/ppermute | solution.py:44
  2046.0 28.0 %collective-permute-start.31 = (f32[512,256]{1,0:T(8,128)}, f32[512,256]{1,0:T(8,128)S(1)}, u32[]{:S(2)}, u32[]{:S(2)}) collective-permute-start(f32[512,256]{1,0:T(8,128)} %bitcast.288), channel_id=1, source_target_pairs={{0,16},{8,24},{16,0},{24,8},{1,17},{9,25},{17,1},{25,9},{2,18},{10... | collective-permute-start | bytes 1572872 | tf_op jit(solution)/shard_map/ppermute | solution.py:44
  2047.7 26.2 %collective-permute-start.30 = (f32[512,256]{1,0:T(8,128)}, f32[512,256]{1,0:T(8,128)S(1)}, u32[]{:S(2)}, u32[]{:S(2)}) collective-permute-start(f32[512,256]{1,0:T(8,128)} %bitcast.289), channel_id=1, source_target_pairs={{0,8},{8,16},{16,24},{24,0},{1,9},{9,17},{17,25},{25,1},{2,10},{10... | collective-permute-start | bytes 1572872 | tf_op jit(solution)/shard_map/ppermute | solution.py:44
Sparse Core Ops, SparseCore 0:
  826.5 74.0 reduce-scatter.18
  902.9 73.1 reduce-scatter.20
  1085.4 67.1 all-gather.3
  1255.2 71.4 reduce-scatter.22
  1328.9 73.1 reduce-scatter.24
  1511.9 67.1 all-gather.5
  1681.7 71.4 reduce-scatter.26
  1755.5 73.1 reduce-scatter.28
  1938.2 67.1 all-gather.7

commit v5 on v4

--- a/solution.py
+++ b/solution.py
@@ -66,14 +66,14 @@
     n_rows, n_ff = gradient.shape
     piece = n_ff // (n_col * n_grad)
     half = piece // HALVES
+    test_rows, gradient = lax.optimization_barrier((grad_gather(test_matrix), gradient))
     split = gradient.reshape(n_rows, n_col, n_grad, HALVES, half)
     chunks = []
     for h in range(HALVES):
         moved = lax.all_to_all(split[:, :, :, h], "grad", split_axis=2, concat_axis=0, tiled=True)
         chunks.append(moved.reshape(n_grad * n_rows, n_col * half))
 
-    def sketch_of(row_piece):
-        rows = grad_gather(row_piece)
+    def sketch_of(rows):
         parts = []
         for chunk in chunks:
             partial = lax.dot_general(
@@ -82,7 +82,7 @@
             parts.append(lax.psum_scatter(partial, "col", scatter_dimension=0, tiled=True))
         return jnp.concatenate(parts, axis=0)
 
-    sketch = sketch_of(test_matrix)
+    sketch = sketch_of(test_rows)
     for iteration in range(POWER + 1):
         basis_rows = orthonormal(sketch)
         basis_bf = lax.all_gather(
@@ -93,7 +93,7 @@
             partial = partial + jnp.dot(chunks[h], basis_bf[h], preferred_element_type=jnp.float32)
         reduced = grad_scatter_sum(partial)
         if iteration < POWER:
-            sketch = sketch_of(reduced.astype(jnp.bfloat16))
+            sketch = sketch_of(grad_gather(reduced.astype(jnp.bfloat16)))
     projector = grad_gather(basis_rows * math.sqrt(FF))
     return (reduced, projector)
 

time: 2090 us -> 1970 us (0.943)
  local copies, waits for them, and re-layouts: 365 us -> 284 us
  waiting for transfers between devices: 1270 us -> 1220 us
    ppermute x12, waiting for transfers between devices: 325 us -> 30 us  [grad_gather(): lax.ppermute(value, 'grad', [(i, (i + s) % size) for i in range(size)])]
    all_to_all x2, waiting for transfers between devices: 277 us -> 504 us  [shards(): lax.all_to_all(split[:, :, :, h], 'grad', split_axis=2, concat_axis=0, ti...]
    unnamed x22 -> x15, local copies, waits for them, and re-layouts: 161 us -> 41.6 us
    optimization_barrier x0 -> x1, local copies, waits for them, and re-layouts: none -> 70.6 us  [shards(): lax.optimization_barrier((grad_gather(test_matrix), gradient))]
    dynamic_slice x15 -> x0, local copies, waits for them, and re-layouts: 26.7 us -> none  [the longest x6 19.5 us: grad_scatter_sum(): total = lax.dynamic_index_in_dim(pieces, index, keepdims=False)]
  transfers between devices with their start and end apart: 47 -> 47, of which waited for: 34 -> 39; matrix products, arithmetic and copies ran while one was open for 14% -> 12% of each run, Pallas kernels for 0% -> 0%
where the time goes in v5:
time: 1970 us; the launch traced here: 1960 us
  waiting for transfers between devices  1220 us (62%)
  local copies, waits for them, and re-layouts  284 us (14%)
  matrix products  192 us (10%)
  other arithmetic  184 us (9%)
  starting transfers between devices  62.6 us (3%)
    all_to_all x2, waiting for transfers between devices, shards(): lax.all_to_all(split[:, :, :, h], 'grad', split_axis=2, concat_axis=0, ti...  504 us
    reduce_scatter x6, waiting for transfers between devices, sketch_of(): lax.psum_scatter(partial, 'col', scatter_dimension=0, tiled=True)  335 us
    all_gather x3, waiting for transfers between devices, shards(): lax.all_gather(basis_rows.astype(jnp.bfloat16).reshape(HALVES, half, -1),...  195 us
    ppermute x15, waiting for transfers between devices, all_sum(): lax.ppermute(value, axis, [(i, i ^ step) for i in range(size)])  108 us
    another operation x20, other arithmetic, orthonormal(): lower_factor = jnp.linalg.cholesky(gram)  104 us
    dot_general x6, matrix products, sketch_of(): lax.dot_general(chunk, rows, (((0,), (0,)), ((), ())), preferred_element_...  93 us
    squeeze x3, local copies, waits for them, and re-layouts, shards(): split[:, :, :, h]  73.4 us
    optimization_barrier x1, local copies, waits for them, and re-layouts, shards(): lax.optimization_barrier((grad_gather(test_matrix), gradient))  70.6 us
  transfers between devices with their start and end apart: 47, of which 39 were waited for; matrix products, arithmetic and copies ran while one was open for 12% of the time, Pallas kernels for 0%

profile of v5, /device:TPU:0, one launch (start us, length us, event | category | flops | bytes accessed | tf_op | source)
XLA Modules:
  0.0 1959.4 jit_solution(17995941877954586183)
XLA Ops:
  26.1 70.6 %copy.29 = bf16[512,53248]{0,1:T(8,128)(2,1)} copy(bf16[512,53248]{1,0:T(8,128)(2,1)} %param.7) | data formatting | bytes 109051904 | tf_op jit(solution)/shard_map/optimization_barrier | solution.py:69
  96.7 35.5 %slice_bitcast_fusion.1 = (bf16[512,8,4,832]{0,3,2,1:T(8,128)(2,1)}, bf16[512,8,4,832]{0,3,2,1:T(8,128)(2,1)}) fusion(bf16[512,8,4,2,832]{0,4,3,2,1:T(8,128)(2,1)} %bitcast.232), kind=kLoop, calls=%fused_computation.7 | loop fusion | bytes 109051904 | tf_op jit(solution)/shard_map/squeeze | solution.py:73
  132.2 18.7 copy.30
  150.9 8.7 all-to-all-start
  159.6 19.2 copy.32
  178.9 275.5 %all-to-all-done = bf16[512,8,4,832]{0,3,1,2:T(8,128)(2,1)} async-done(((bf16[512,8,4,832]{0,3,1,2:T(8,128)(2,1)}), bf16[512,8,4,832]{0,3,1,2:T(8,128)(2,1)}, u32[]{:S(2)}, u32[]{:S(2)}) %all-to-all-start) | async-done | bytes 27263008 | tf_op jit(solution)/shard_map/all_to_all | solution.py:73
  454.4 8.7 all-to-all-start.1
  463.2 31.4 %copy.31 = bf16[4,512,8,1,832]{1,0,4,2,3:T(4,128)(2,1)} copy(bf16[4,512,8,1,832]{1,4,2,0,3:T(8,128)(2,1)} %bitcast.8) | data formatting | bytes 54525952 | tf_op jit(solution)/shard_map/all_to_all | solution.py:73
  494.5 19.0 copy.50
  513.6 15.4 fusion.59
  529.2 228.0 %all-to-all-done.1 = bf16[512,8,4,832]{0,3,1,2:T(8,128)(2,1)} async-done(((bf16[512,8,4,832]{0,3,1,2:T(8,128)(2,1)}), bf16[512,8,4,832]{0,3,1,2:T(8,128)(2,1)}, u32[]{:S(2)}, u32[]{:S(2)}) %all-to-all-start.1) | async-done | bytes 27263008 | tf_op jit(solution)/shard_map/all_to_all | solution.py:73
  757.2 31.4 %copy.33 = bf16[4,512,8,1,832]{1,0,4,2,3:T(4,128)(2,1)} copy(bf16[4,512,8,1,832]{1,4,2,0,3:T(8,128)(2,1)} %bitcast.11) | data formatting | bytes 54525952 | tf_op jit(solution)/shard_map/all_to_all | solution.py:73
  788.6 18.9 copy.51
  807.5 15.2 fusion.60
  824.3 73.8 %reduce-scatter.9.cloned.1.call-done = f32[832,256]{1,0:T(8,128)} async-done(((f32[6656,256]{1,0:T(8,128)}), f32[832,256]{1,0:T(8,128)}) %reduce-scatter.9.cloned.1.call-update) | async-done | bytes 851984 | tf_op jit(solution)/shard_map/reduce_scatter | solution.py:82
  903.9 8.3 collective-permute-done.4
  912.9 13.4 collective-permute-done.5
  927.9 6.7 collective-permute-done.6
  936.2 5.9 collective-permute-done.7
  942.3 11.7 cholesky.172
  954.1 9.8 custom-call.15
  964.4 12.2 cholesky.189
  982.6 19.7 %custom-call.16 = f32[2,128,128]{1,2,0:T(8,128)S(1)} custom-call(f32[2,128,128]{2,1,0:T(8,128)S(1)} %get-tuple-element.29), custom_call_target="InvertDiagBlocksLowerTriangular" | custom-call | tf_op jit(solution)/shard_map/triangular_solve/custom-call.0 | solution.py:58
  1007.4 67.1 %all-gather.4.cloned.1.call-done = bf16[2,6656,256]{2,1,0:T(8,128)(2,1)} async-done(((bf16[2,832,256]{2,1,0:T(8,128)(2,1)}), bf16[2,6656,256]{2,1,0:T(8,128)(2,1)}) %all-gather.4.cloned.1.call-update) | async-done | bytes 6815760 | tf_op jit(solution)/shard_map/all_gather | solution.py:88
  1074.5 13.6 fusion.5
  1088.1 12.5 fusion.7
  1105.2 11.5 collective-permute-done.10
  1116.8 11.6 collective-permute-done.8
  1134.5 6.1 collective-permute-done.11
  1144.7 15.4 fusion.62
  1160.1 15.9 fusion.63
  1176.5 56.5 %reduce-scatter.11.cloned.1.call-done = f32[832,256]{1,0:T(8,128)} async-done(((f32[6656,256]{1,0:T(8,128)}), f32[832,256]{1,0:T(8,128)}) %reduce-scatter.11.cloned.1.call-update) | async-done | bytes 851984 | tf_op jit(solution)/shard_map/reduce_scatter | solution.py:82
  1234.1 74.1 %reduce-scatter.13.cloned.1.call-done = f32[832,256]{1,0:T(8,128)} async-done(((f32[6656,256]{1,0:T(8,128)}), f32[832,256]{1,0:T(8,128)}) %reduce-scatter.13.cloned.1.call-update) | async-done | bytes 851984 | tf_op jit(solution)/shard_map/reduce_scatter | solution.py:82
  1314.0 8.3 collective-permute-done.15
  1323.1 13.4 collective-permute-done.16
  1338.1 6.7 collective-permute-done.17
  1346.4 5.9 collective-permute-done.18
  1352.5 11.7 cholesky.206
  1364.3 9.8 custom-call.17
  1374.6 11.9 cholesky.223
  1393.1 19.7 %custom-call.18 = f32[2,128,128]{1,2,0:T(8,128)S(1)} custom-call(f32[2,128,128]{2,1,0:T(8,128)S(1)} %get-tuple-element.30), custom_call_target="InvertDiagBlocksLowerTriangular" | custom-call | tf_op jit(solution)/shard_map/triangular_solve/custom-call.0 | solution.py:58
  1417.9 67.1 %all-gather.6.cloned.1.call-done = bf16[2,6656,256]{2,1,0:T(8,128)(2,1)} async-done(((bf16[2,832,256]{2,1,0:T(8,128)(2,1)}), bf16[2,6656,256]{2,1,0:T(8,128)(2,1)}) %all-gather.6.cloned.1.call-update) | async-done | bytes 6815760 | tf_op jit(solution)/shard_map/all_gather | solution.py:88
  1484.9 13.6 fusion.3
  1498.6 12.5 fusion.8
  1515.6 11.3 collective-permute-done.19
  1527.0 10.5 collective-permute-done.20
  1553.1 15.3 fusion.65
  1568.5 15.9 fusion.66
  1584.6 56.6 %reduce-scatter.15.cloned.1.call-done = f32[832,256]{1,0:T(8,128)} async-done(((f32[6656,256]{1,0:T(8,128)}), f32[832,256]{1,0:T(8,128)}) %reduce-scatter.15.cloned.1.call-update) | async-done | bytes 851984 | tf_op jit(solution)/shard_map/reduce_scatter | solution.py:82
  1642.4 74.3 %reduce-scatter.17.cloned.1.call-done = f32[832,256]{1,0:T(8,128)} async-done(((f32[6656,256]{1,0:T(8,128)}), f32[832,256]{1,0:T(8,128)}) %reduce-scatter.17.cloned.1.call-update) | async-done | bytes 851984 | tf_op jit(solution)/shard_map/reduce_scatter | solution.py:82
  1722.5 8.3 collective-permute-done.26
  1731.5 13.4 collective-permute-done.27
  1746.5 6.8 collective-permute-done.28
  1754.8 5.9 collective-permute-done.29
  1761.0 11.7 cholesky.240
  1772.7 9.8 custom-call.19
  1783.0 11.9 cholesky.257
  1801.6 19.7 %custom-call.20 = f32[2,128,128]{1,2,0:T(8,128)S(1)} custom-call(f32[2,128,128]{2,1,0:T(8,128)S(1)} %get-tuple-element.31), custom_call_target="InvertDiagBlocksLowerTriangular" | custom-call | tf_op jit(solution)/shard_map/triangular_solve/custom-call.0 | solution.py:58
  1832.8 60.7 %all-gather.8.cloned.1.call-done = bf16[2,6656,256]{2,1,0:T(8,128)(2,1)} async-done(((bf16[2,832,256]{2,1,0:T(8,128)(2,1)}), bf16[2,6656,256]{2,1,0:T(8,128)(2,1)}) %all-gather.8.cloned.1.call-update) | async-done | bytes 6815760 | tf_op jit(solution)/shard_map/all_gather | solution.py:88
  1893.5 13.6 fusion.1
  1907.1 12.5 fusion.9
  1929.7 6.2 rev.15
  1935.9 6.6 fusion
  1942.4 7.6 copy.46
  (198 shorter events, 151.1 us)
Async XLA Ops:
  7.2 11.4 collective-permute-start
  10.2 13.1 collective-permute-start.1
  11.7 11.9 collective-permute-start.2
  150.9 303.5 %all-to-all-start = ((bf16[512,8,4,832]{0,3,1,2:T(8,128)(2,1)}), bf16[512,8,4,832]{0,3,1,2:T(8,128)(2,1)}, u32[]{:S(2)}, u32[]{:S(2)}) async-start(bf16[512,8,4,832]{0,3,1,2:T(8,128)(2,1)} %copy.30), calls=%async_computation | async-start | bytes 54525952 | tf_op jit(solution)/shard_map/all_to_all | solution.py:73
  454.4 302.8 %all-to-all-start.1 = ((bf16[512,8,4,832]{0,3,1,2:T(8,128)(2,1)}), bf16[512,8,4,832]{0,3,1,2:T(8,128)(2,1)}, u32[]{:S(2)}, u32[]{:S(2)}) async-start(bf16[512,8,4,832]{0,3,1,2:T(8,128)(2,1)} %copy.32), calls=%async_computation.2 | async-start | bytes 54525952 | tf_op jit(solution)/shard_map/all_to_all | solution.py:73
  463.1 359.9 %reduce-scatter.7.cloned.1.call-start = ((), (), s32[]{:S(2)}) async-start(), calls=%async_computation.8 | async-start | bytes 7667712 | tf_op jit(solution)/shard_map/reduce_scatter | solution.py:82
  494.5 19.0 copy-start.1
  529.0 369.1 %reduce-scatter.9.cloned.1.call-start = ((), (), s32[]{:S(2)}) async-start(), calls=%async_computation.9 | async-start | bytes 7667712 | tf_op jit(solution)/shard_map/reduce_scatter | solution.py:82
  822.7 251.8 %all-gather.4.cloned.1.call-start = ((), (), s32[]{:S(2)}) async-start(), calls=%async_computation.10 | async-start | bytes 7667712 | tf_op jit(solution)/shard_map/all_gather | solution.py:88
  902.1 1.6 collective-permute-start.3
  903.8 8.4 collective-permute-start.4
  912.2 14.1 collective-permute-start.5
  926.3 8.3 collective-permute-start.6
  934.7 7.4 collective-permute-start.7
  1007.2 225.8 %reduce-scatter.11.cloned.1.call-start = ((), (), s32[]{:S(2)}) async-start(), calls=%async_computation.11 | async-start | bytes 7667712 | tf_op jit(solution)/shard_map/reduce_scatter | solution.py:82
  1074.5 13.6 copy-start.2
  1101.7 15.0 collective-permute-start.10
  1104.1 24.2 %collective-permute-start.8 = (f32[512,256]{1,0:T(8,128)}, f32[512,256]{1,0:T(8,128)}, u32[]{:S(2)}, u32[]{:S(2)}) collective-permute-start(f32[512,256]{1,0:T(8,128)} %get-tuple-element.70), channel_id=1, source_target_pairs={{0,8},{8,16},{16,24},{24,0},{1,9},{9,17},{17,25},{25,1},{2,10},{10... | collective-permute-start | bytes 1572872 | tf_op jit(solution)/shard_map/ppermute | solution.py:44
  1104.1 25.1 %collective-permute-start.9 = (f32[512,256]{1,0:T(8,128)S(1)}, f32[512,256]{1,0:T(8,128)}, u32[]{:S(2)}, u32[]{:S(2)}) collective-permute-start(f32[512,256]{1,0:T(8,128)S(1)} %get-tuple-element.72), channel_id=1, source_target_pairs={{0,16},{8,24},{16,0},{24,8},{1,17},{9,25},{17,1},{25,9},{2,18},{10... | collective-permute-start | bytes 1572872 | tf_op jit(solution)/shard_map/ppermute | solution.py:44
  1130.5 10.2 collective-permute-start.11
  1131.1 13.0 collective-permute-start.12
  1132.5 11.5 collective-permute-start.13
  1160.1 148.2 %reduce-scatter.13.cloned.1.call-start = ((), (), s32[]{:S(2)}) async-start(), calls=%async_computation.12 | async-start | bytes 7667712 | tf_op jit(solution)/shard_map/reduce_scatter | solution.py:82
  1176.0 308.9 %all-gather.6.cloned.1.call-start = ((), (), s32[]{:S(2)}) async-start(), calls=%async_computation.13 | async-start | bytes 7667712 | tf_op jit(solution)/shard_map/all_gather | solution.py:88
  1312.3 1.6 collective-permute-start.14
  1314.0 8.4 collective-permute-start.15
  1322.4 14.1 collective-permute-start.16
  1336.5 8.3 collective-permute-start.17
  1344.9 7.4 collective-permute-start.18
  1417.6 223.6 %reduce-scatter.15.cloned.1.call-start = ((), (), s32[]{:S(2)}) async-start(), calls=%async_computation.14 | async-start | bytes 7667712 | tf_op jit(solution)/shard_map/reduce_scatter | solution.py:82
  1484.9 13.6 copy-start.4
  1511.2 15.8 collective-permute-start.19
  1512.7 24.7 %collective-permute-start.20 = (f32[512,256]{1,0:T(8,128)S(1)}, f32[512,256]{1,0:T(8,128)S(1)}, u32[]{:S(2)}, u32[]{:S(2)}) collective-permute-start(f32[512,256]{1,0:T(8,128)S(1)} %get-tuple-element.69), channel_id=1, source_target_pairs={{0,16},{8,24},{16,0},{24,8},{1,17},{9,25},{17,1},{25,9},{2,18},{10... | collective-permute-start | bytes 1572872 | tf_op jit(solution)/shard_map/ppermute | solution.py:44
  1514.2 23.3 %collective-permute-start.21 = (f32[512,256]{1,0:T(8,128)S(1)}, f32[512,256]{1,0:T(8,128)S(1)}, u32[]{:S(2)}, u32[]{:S(2)}) collective-permute-start(f32[512,256]{1,0:T(8,128)S(1)} %get-tuple-element.68), channel_id=1, source_target_pairs={{0,24},{8,0},{16,8},{24,16},{1,25},{9,1},{17,9},{25,17},{2,26},{10... | collective-permute-start | bytes 1572872 | tf_op jit(solution)/shard_map/ppermute | solution.py:44
  1537.6 10.1 collective-permute-start.22
  1539.4 12.7 collective-permute-start.23
  1540.0 12.5 collective-permute-start.24
  1568.4 148.3 %reduce-scatter.17.cloned.1.call-start = ((), (), s32[]{:S(2)}) async-start(), calls=%async_computation.15 | async-start | bytes 7667712 | tf_op jit(solution)/shard_map/reduce_scatter | solution.py:82
  1584.4 309.1 %all-gather.8.cloned.1.call-start = ((), (), s32[]{:S(2)}) async-start(), calls=%async_computation.16 | async-start | bytes 7667712 | tf_op jit(solution)/shard_map/all_gather | solution.py:88
  1720.8 1.6 collective-permute-start.25
  1722.4 8.4 collective-permute-start.26
  1730.9 14.1 collective-permute-start.27
  1745.0 8.3 collective-permute-start.28
  1753.3 7.4 collective-permute-start.29
  1828.1 95.3 %collective-permute-start.33 = (f32[1664,256]{0,1:T(8,128)}, f32[1664,256]{0,1:T(8,128)}, u32[]{:S(2)}, u32[]{:S(2)}) collective-permute-start(f32[1664,256]{0,1:T(8,128)} %get-tuple-element.74), channel_id=1, source_target_pairs={{0,8},{8,16},{16,24},{24,0},{1,9},{9,17},{17,25},{25,1},{2,10},{10... | collective-permute-start | bytes 5111816 | tf_op jit(solution)/shard_map/ppermute | solution.py:30
  1829.6 95.3 %collective-permute-start.34 = (f32[1664,256]{0,1:T(8,128)}, f32[1664,256]{0,1:T(8,128)}, u32[]{:S(2)}, u32[]{:S(2)}) collective-permute-start(f32[1664,256]{0,1:T(8,128)} %get-tuple-element.74), channel_id=1, source_target_pairs={{0,16},{8,24},{16,0},{24,8},{1,17},{9,25},{17,1},{25,9},{2,18},{10... | collective-permute-start | bytes 5111816 | tf_op jit(solution)/shard_map/ppermute | solution.py:30
  1831.1 93.9 %collective-permute-start.35 = (f32[1664,256]{0,1:T(8,128)}, f32[1664,256]{0,1:T(8,128)}, u32[]{:S(2)}, u32[]{:S(2)}) collective-permute-start(f32[1664,256]{0,1:T(8,128)} %get-tuple-element.74), channel_id=1, source_target_pairs={{0,24},{8,0},{16,8},{24,16},{1,25},{9,1},{17,9},{25,17},{2,26},{10... | collective-permute-start | bytes 5111816 | tf_op jit(solution)/shard_map/ppermute | solution.py:30
  1893.5 13.6 copy-start.3
  1919.6 5.4 copy-start
  1920.5 29.6 %collective-permute-start.30 = (f32[512,256]{1,0:T(8,128)}, f32[512,256]{1,0:T(8,128)}, u32[]{:S(2)}, u32[]{:S(2)}) collective-permute-start(f32[512,256]{1,0:T(8,128)} %get-tuple-element.64), channel_id=1, source_target_pairs={{0,8},{8,16},{16,24},{24,0},{1,9},{9,17},{17,25},{25,1},{2,10},{10... | collective-permute-start | bytes 1572872 | tf_op jit(solution)/shard_map/ppermute | solution.py:44
  1922.0 28.1 %collective-permute-start.31 = (f32[512,256]{1,0:T(8,128)S(1)}, f32[512,256]{1,0:T(8,128)}, u32[]{:S(2)}, u32[]{:S(2)}) collective-permute-start(f32[512,256]{1,0:T(8,128)S(1)} %get-tuple-element.66), channel_id=1, source_target_pairs={{0,16},{8,24},{16,0},{24,8},{1,17},{9,25},{17,1},{25,9},{2,18},{10... | collective-permute-start | bytes 1572872 | tf_op jit(solution)/shard_map/ppermute | solution.py:44
  1923.5 26.6 %collective-permute-start.32 = (f32[512,256]{1,0:T(8,128)S(1)}, f32[512,256]{1,0:T(8,128)}, u32[]{:S(2)}, u32[]{:S(2)}) collective-permute-start(f32[512,256]{1,0:T(8,128)S(1)} %get-tuple-element.65), channel_id=1, source_target_pairs={{0,24},{8,0},{16,8},{24,16},{1,25},{9,1},{17,9},{25,17},{2,26},{10... | collective-permute-start | bytes 1572872 | tf_op jit(solution)/shard_map/ppermute | solution.py:44
Sparse Core Ops, SparseCore 0:
  529.1 76.4 reduce-scatter.6
  822.8 75.1 reduce-scatter.8
  1007.3 67.1 all-gather.3
  1160.2 72.7 reduce-scatter.10
  1235.1 73.1 reduce-scatter.12
  1417.8 67.1 all-gather.5
  1568.6 72.5 reduce-scatter.14
  1643.5 73.1 reduce-scatter.16
  1826.3 67.1 all-gather.7

commit v6 on v5

--- a/solution.py
+++ b/solution.py
@@ -34,13 +34,21 @@
     return ordered.reshape((size * value.shape[0],) + value.shape[1:])
 
 
-def grad_scatter_sum(value):
+def shift_gather(value):
     size = lax.axis_size("grad")
-    index = lax.axis_index("grad")
+    received = [value] + [
+        lax.ppermute(value, "grad", [(i, (i + s) % size) for i in range(size)])
+        for s in range(1, size)
+    ]
+    return jnp.concatenate(received, axis=0)
+
+
+def shift_scatter_sum(value):
+    size = lax.axis_size("grad")
     pieces = value.reshape((size, value.shape[0] // size) + value.shape[1:])
-    total = lax.dynamic_index_in_dim(pieces, index, keepdims=False)
+    total = pieces[0]
     for s in range(1, size):
-        outgoing = lax.dynamic_index_in_dim(pieces, (index + s) % size, keepdims=False)
+        outgoing = pieces[(size - s) % size]
         total = total + lax.ppermute(outgoing, "grad", [(i, (i + s) % size) for i in range(size)])
     return total
 
@@ -66,11 +74,19 @@
     n_rows, n_ff = gradient.shape
     piece = n_ff // (n_col * n_grad)
     half = piece // HALVES
-    test_rows, gradient = lax.optimization_barrier((grad_gather(test_matrix), gradient))
+    test_rows, gradient = lax.optimization_barrier((shift_gather(test_matrix), gradient))
+    index = lax.axis_index("grad")
     split = gradient.reshape(n_rows, n_col, n_grad, HALVES, half)
     chunks = []
     for h in range(HALVES):
-        moved = lax.all_to_all(split[:, :, :, h], "grad", split_axis=2, concat_axis=0, tiled=True)
+        part = split[:, :, :, h]
+        received = [lax.dynamic_index_in_dim(part, index, axis=2, keepdims=False)]
+        for s in range(1, n_grad):
+            outgoing = lax.dynamic_index_in_dim(part, (index + s) % n_grad, axis=2, keepdims=False)
+            received.append(
+                lax.ppermute(outgoing, "grad", [(i, (i + s) % n_grad) for i in range(n_grad)])
+            )
+        moved = jnp.concatenate(received, axis=0)
         chunks.append(moved.reshape(n_grad * n_rows, n_col * half))
 
     def sketch_of(rows):
@@ -91,9 +107,9 @@
         partial = jnp.dot(chunks[0], basis_bf[0], preferred_element_type=jnp.float32)
         for h in range(1, HALVES):
             partial = partial + jnp.dot(chunks[h], basis_bf[h], preferred_element_type=jnp.float32)
-        reduced = grad_scatter_sum(partial)
+        reduced = shift_scatter_sum(partial)
         if iteration < POWER:
-            sketch = sketch_of(grad_gather(reduced.astype(jnp.bfloat16)))
+            sketch = sketch_of(shift_gather(reduced.astype(jnp.bfloat16)))
     projector = grad_gather(basis_rows * math.sqrt(FF))
     return (reduced, projector)
 

time: 1970 us -> 1960 us (level)
  local copies, waits for them, and re-layouts: 284 us -> 174 us
  waiting for transfers between devices: 1220 us -> 1300 us
  other arithmetic: 184 us -> 218 us
    ppermute x9 -> x24, waiting for transfers between devices: 45.9 us -> 665 us  [the longest x6 583 us: shards(): lax.ppermute(outgoing, 'grad', [(i, (i + s) % n_grad) for i in range(n_gr...]
    all_to_all x2 -> x0, waiting for transfers between devices: 504 us -> none  [shards(): lax.all_to_all(split[:, :, :, h], 'grad', split_axis=2, concat_axis=0, ti...]
    squeeze x6 -> x0, local copies, waits for them, and re-layouts: 75.6 us -> none  [the longest x3 73.4 us: shards(): split[:, :, :, h]]
    all_to_all x2 -> x0, local copies, waits for them, and re-layouts: 62.8 us -> none  [shards(): lax.all_to_all(split[:, :, :, h], 'grad', split_axis=2, concat_axis=0, ti...]
    concatenate x0 -> x3, other arithmetic: none -> 38.2 us  [the longest x2 37.1 us: shards(): moved = jnp.concatenate(received, axis=0)]
    slice x0 -> x4, local copies, waits for them, and re-layouts: none -> 37 us  [the longest x1 35.6 us: shards(): part = split[:, :, :, h]]
    ppermute x12 -> x3, waiting for transfers between devices: 30 us -> 0.01 us  [grad_gather(): lax.ppermute(value, 'grad', [(i, (i + s) % size) for i in range(size)])]
    unnamed x15 -> x23, local copies, waits for them, and re-layouts: 41.6 us -> 13.3 us
  transfers between devices with their start and end apart: 47 -> 51, of which waited for: 39 -> 37; matrix products, arithmetic and copies ran while one was open for 12% -> 7% of each run, Pallas kernels for 0% -> 0%
where the time goes in v6:
time: 1960 us; the launch traced here: 1950 us
  waiting for transfers between devices  1300 us (66%)
  other arithmetic  218 us (11%)
  matrix products  198 us (10%)
  local copies, waits for them, and re-layouts  174 us (9%)
  starting transfers between devices  43.5 us (2%)
    ppermute x6, waiting for transfers between devices, shards(): lax.ppermute(outgoing, 'grad', [(i, (i + s) % n_grad) for i in range(n_gr...  583 us
    reduce_scatter x6, waiting for transfers between devices, sketch_of(): lax.psum_scatter(partial, 'col', scatter_dimension=0, tiled=True)  331 us
    all_gather x3, waiting for transfers between devices, shards(): lax.all_gather(basis_rows.astype(jnp.bfloat16).reshape(HALVES, half, -1),...  196 us
    ppermute x15, waiting for transfers between devices, all_sum(): lax.ppermute(value, axis, [(i, i ^ step) for i in range(size)])  108 us
    another operation x20, other arithmetic, orthonormal(): lower_factor = jnp.linalg.cholesky(gram)  104 us
    dot_general x6, matrix products, sketch_of(): lax.dot_general(chunk, rows, (((0,), (0,)), ((), ())), preferred_element_...  99.8 us
    optimization_barrier x1, local copies, waits for them, and re-layouts, shards(): lax.optimization_barrier((shift_gather(test_matrix), gradient))  64.7 us
    another operation x7, other arithmetic, orthonormal(): lax.linalg.triangular_solve(lower_factor, rows, left_side=False, lower=Tr...  59.1 us
  transfers between devices with their start and end apart: 51, of which 37 were waited for; matrix products, arithmetic and copies ran while one was open for 7% of the time, Pallas kernels for 0%

profile of v6, /device:TPU:0, one launch (start us, length us, event | category | flops | bytes accessed | tf_op | source)
XLA Modules:
  0.0 1951.5 jit_solution(17630761638626761423)
XLA Ops:
  12.3 5.9 collective-permute-done.2
  18.2 6.6 collective-permute-done.1
  25.8 64.7 %copy.13 = bf16[512,53248]{0,1:T(8,128)(2,1)} copy(bf16[512,53248]{1,0:T(8,128)(2,1)} %param.5) | data formatting | bytes 109051904 | tf_op jit(solution)/shard_map/optimization_barrier | solution.py:77
  90.5 35.6 %fusion.64 = (bf16[512,8,4,1,832]{0,4,3,2,1:T(8,128)(2,1)}, bf16[512,8,4,1,832]{0,4,3,2,1:T(8,128)(2,1)}) fusion(bf16[512,8,4,2,832]{0,4,3,2,1:T(8,128)(2,1)} %bitcast.170), kind=kLoop, calls=%fused_computation.143 | loop fusion | bytes 109051904 | tf_op jit(solution)/shard_map/slice | solution.py:82
  126.1 12.3 constant_dynamic-slice_fusion.4
  141.0 147.1 %collective-permute-done.5 = bf16[512,8,832]{0,2,1:T(8,128)(2,1)S(1)} collective-permute-done((bf16[512,8,832]{0,2,1:T(8,128)(2,1)S(1)}, bf16[512,8,832]{0,2,1:T(8,128)(2,1)S(1)}, u32[]{:S(2)}, u32[]{:S(2)}) %collective-permute-start.5) | collective-permute-done | bytes 6815776 | tf_op jit(solution)/shard_map/ppermute | solution.py:87
  288.1 144.7 %collective-permute-done.4 = bf16[512,8,832]{0,2,1:T(8,128)(2,1)S(1)} collective-permute-done((bf16[512,8,832]{0,2,1:T(8,128)(2,1)S(1)}, bf16[512,8,832]{0,2,1:T(8,128)(2,1)S(1)}, u32[]{:S(2)}, u32[]{:S(2)}) %collective-permute-start.4) | collective-permute-done | bytes 6815776 | tf_op jit(solution)/shard_map/ppermute | solution.py:87
  437.7 18.6 pad_maximum_fusion
  456.3 15.3 fusion.68
  471.6 12.9 constant_dynamic-slice_fusion.3
  487.2 147.0 %collective-permute-done.8 = bf16[512,8,832]{0,2,1:T(8,128)(2,1)S(1)} collective-permute-done((bf16[512,8,832]{0,2,1:T(8,128)(2,1)S(1)}, bf16[512,8,832]{0,2,1:T(8,128)(2,1)S(1)}, u32[]{:S(2)}, u32[]{:S(2)}) %collective-permute-start.8) | collective-permute-done | bytes 6815776 | tf_op jit(solution)/shard_map/ppermute | solution.py:87
  634.2 144.5 %collective-permute-done.7 = bf16[512,8,832]{0,2,1:T(8,128)(2,1)S(1)} collective-permute-done((bf16[512,8,832]{0,2,1:T(8,128)(2,1)S(1)}, bf16[512,8,832]{0,2,1:T(8,128)(2,1)S(1)}, u32[]{:S(2)}, u32[]{:S(2)}) %collective-permute-start.7) | collective-permute-done | bytes 6815776 | tf_op jit(solution)/shard_map/ppermute | solution.py:87
  783.5 18.6 pad_maximum_fusion.1
  802.1 15.4 fusion.69
  818.9 73.7 %reduce-scatter.9.cloned.1.call-done = f32[832,256]{1,0:T(8,128)} async-done(((f32[6656,256]{1,0:T(8,128)}), f32[832,256]{1,0:T(8,128)}) %reduce-scatter.9.cloned.1.call-update) | async-done | bytes 851984 | tf_op jit(solution)/shard_map/reduce_scatter | solution.py:98
  898.4 8.3 collective-permute-done.10
  907.4 13.4 collective-permute-done.11
  922.4 6.8 collective-permute-done.12
  936.9 11.7 cholesky.172
  948.7 9.8 custom-call.15
  959.0 12.1 cholesky.189
  977.1 19.7 %custom-call.16 = f32[2,128,128]{1,2,0:T(8,128)S(1)} custom-call(f32[2,128,128]{2,1,0:T(8,128)S(1)} %get-tuple-element.28), custom_call_target="InvertDiagBlocksLowerTriangular" | custom-call | tf_op jit(solution)/shard_map/triangular_solve/custom-call.0 | solution.py:66
  1001.8 67.1 %all-gather.4.cloned.1.call-done = bf16[2,6656,256]{2,1,0:T(8,128)(2,1)} async-done(((bf16[2,832,256]{2,1,0:T(8,128)(2,1)}), bf16[2,6656,256]{2,1,0:T(8,128)(2,1)}) %all-gather.4.cloned.1.call-update) | async-done | bytes 6815760 | tf_op jit(solution)/shard_map/all_gather | solution.py:104
  1068.9 13.6 fusion.5
  1082.5 12.5 fusion.7
  1098.7 11.3 collective-permute-done.16
  1110.0 12.6 collective-permute-done.15
  1125.6 6.4 collective-permute-done.19
  1136.3 17.0 fusion.32
  1153.4 17.6 fusion.31
  1171.4 54.2 %reduce-scatter.11.cloned.1.call-done = f32[832,256]{1,0:T(8,128)} async-done(((f32[6656,256]{1,0:T(8,128)}), f32[832,256]{1,0:T(8,128)}) %reduce-scatter.11.cloned.1.call-update) | async-done | bytes 851984 | tf_op jit(solution)/shard_map/reduce_scatter | solution.py:98
  1226.9 74.1 %reduce-scatter.13.cloned.1.call-done = f32[832,256]{1,0:T(8,128)} async-done(((f32[6656,256]{1,0:T(8,128)}), f32[832,256]{1,0:T(8,128)}) %reduce-scatter.13.cloned.1.call-update) | async-done | bytes 851984 | tf_op jit(solution)/shard_map/reduce_scatter | solution.py:98
  1306.7 8.3 collective-permute-done.21
  1315.8 13.4 collective-permute-done.22
  1330.8 6.8 collective-permute-done.23
  1339.1 5.9 collective-permute-done.24
  1345.2 11.7 cholesky.206
  1357.0 9.8 custom-call.17
  1367.3 11.9 cholesky.223
  1385.7 19.7 %custom-call.18 = f32[2,128,128]{1,2,0:T(8,128)S(1)} custom-call(f32[2,128,128]{2,1,0:T(8,128)S(1)} %get-tuple-element.29), custom_call_target="InvertDiagBlocksLowerTriangular" | custom-call | tf_op jit(solution)/shard_map/triangular_solve/custom-call.0 | solution.py:66
  1410.5 67.1 %all-gather.6.cloned.1.call-done = bf16[2,6656,256]{2,1,0:T(8,128)(2,1)} async-done(((bf16[2,832,256]{2,1,0:T(8,128)(2,1)}), bf16[2,6656,256]{2,1,0:T(8,128)(2,1)}) %all-gather.6.cloned.1.call-update) | async-done | bytes 6815760 | tf_op jit(solution)/shard_map/all_gather | solution.py:104
  1477.6 13.6 fusion.3
  1491.2 12.5 fusion.8
  1507.4 11.3 collective-permute-done.27
  1518.7 12.6 collective-permute-done.26
  1534.4 6.2 collective-permute-done.30
  1545.0 17.0 fusion.30
  1562.0 17.6 fusion.29
  1579.9 54.4 %reduce-scatter.15.cloned.1.call-done = f32[832,256]{1,0:T(8,128)} async-done(((f32[6656,256]{1,0:T(8,128)}), f32[832,256]{1,0:T(8,128)}) %reduce-scatter.15.cloned.1.call-update) | async-done | bytes 851984 | tf_op jit(solution)/shard_map/reduce_scatter | solution.py:98
  1635.5 74.3 %reduce-scatter.17.cloned.1.call-done = f32[832,256]{1,0:T(8,128)} async-done(((f32[6656,256]{1,0:T(8,128)}), f32[832,256]{1,0:T(8,128)}) %reduce-scatter.17.cloned.1.call-update) | async-done | bytes 851984 | tf_op jit(solution)/shard_map/reduce_scatter | solution.py:98
  1715.6 8.3 collective-permute-done.32
  1724.6 13.4 collective-permute-done.33
  1739.6 6.8 collective-permute-done.34
  1747.9 5.9 collective-permute-done.35
  1754.0 11.7 cholesky.240
  1765.8 9.8 custom-call.19
  1776.1 11.9 cholesky.257
  1794.6 19.7 %custom-call.20 = f32[2,128,128]{1,2,0:T(8,128)S(1)} custom-call(f32[2,128,128]{2,1,0:T(8,128)S(1)} %get-tuple-element.30), custom_call_target="InvertDiagBlocksLowerTriangular" | custom-call | tf_op jit(solution)/shard_map/triangular_solve/custom-call.0 | solution.py:66
  1824.9 61.6 %all-gather.8.cloned.1.call-done = bf16[2,6656,256]{2,1,0:T(8,128)(2,1)} async-done(((bf16[2,832,256]{2,1,0:T(8,128)(2,1)}), bf16[2,6656,256]{2,1,0:T(8,128)(2,1)}) %all-gather.8.cloned.1.call-update) | async-done | bytes 6815760 | tf_op jit(solution)/shard_map/all_gather | solution.py:104
  1886.5 13.6 fusion.1
  1900.1 12.6 fusion.9
  1922.2 6.2 rev.3
  1928.4 6.6 fusion
  1934.9 7.6 copy.26
  (206 shorter events, 143.7 us)
Async XLA Ops:
  7.2 810.6 %reduce-scatter.7.cloned.1.call-start = ((), (), s32[]{:S(2)}) async-start(), calls=%async_computation.6 | async-start | bytes 7667712 | tf_op jit(solution)/shard_map/reduce_scatter | solution.py:98
  7.2 11.0 collective-permute-start.2
  11.2 13.6 collective-permute-start.1
  11.7 13.1 collective-permute-start
  138.5 149.6 %collective-permute-start.5 = (bf16[512,8,832]{0,2,1:T(8,128)(2,1)S(1)}, bf16[512,8,832]{0,2,1:T(8,128)(2,1)S(1)}, u32[]{:S(2)}, u32[]{:S(2)}) collective-permute-start(bf16[512,8,832]{0,2,1:T(8,128)(2,1)S(1)} %get-tuple-element.64), channel_id=1, source_target_pairs={{0,24},{8,0},{16,8},{24,16},{1,25},{9,1},{17,9},{25,17},{2,26},{10... | collective-permute-start | bytes 20447240 | tf_op jit(solution)/shard_map/ppermute | solution.py:87
  139.0 293.8 %collective-permute-start.4 = (bf16[512,8,832]{0,2,1:T(8,128)(2,1)S(1)}, bf16[512,8,832]{0,2,1:T(8,128)(2,1)S(1)}, u32[]{:S(2)}, u32[]{:S(2)}) collective-permute-start(bf16[512,8,832]{0,2,1:T(8,128)(2,1)S(1)} %get-tuple-element.65), channel_id=1, source_target_pairs={{0,16},{8,24},{16,0},{24,8},{1,17},{9,25},{17,1},{25,9},{2,18},{10... | collective-permute-start | bytes 20447240 | tf_op jit(solution)/shard_map/ppermute | solution.py:87
  140.2 292.6 %collective-permute-start.3 = (bf16[512,8,832]{0,2,1:T(8,128)(2,1)S(1)}, bf16[512,8,832]{0,2,1:T(8,128)(2,1)S(1)}, u32[]{:S(2)}, u32[]{:S(2)}) collective-permute-start(bf16[512,8,832]{0,2,1:T(8,128)(2,1)S(1)} %get-tuple-element.66), channel_id=1, source_target_pairs={{0,8},{8,16},{16,24},{24,0},{1,9},{9,17},{17,25},{25,1},{2,10},{10... | collective-permute-start | bytes 20447240 | tf_op jit(solution)/shard_map/ppermute | solution.py:87
  288.1 144.7 %copy-start.1 = (bf16[512,8,832]{0,2,1:T(8,128)(2,1)}, bf16[512,8,832]{0,2,1:T(8,128)(2,1)S(1)}, u32[]{:S(2)}) copy-start(bf16[512,8,832]{0,2,1:T(8,128)(2,1)S(1)} %collective-permute-done.5) | copy-start | bytes 20447236
  432.8 2.7 copy-start.3
  432.8 4.9 copy-start.5
  471.6 421.0 %reduce-scatter.9.cloned.1.call-start = ((), (), s32[]{:S(2)}) async-start(), calls=%async_computation.7 | async-start | bytes 7667712 | tf_op jit(solution)/shard_map/reduce_scatter | solution.py:98
  484.6 149.6 %collective-permute-start.8 = (bf16[512,8,832]{0,2,1:T(8,128)(2,1)S(1)}, bf16[512,8,832]{0,2,1:T(8,128)(2,1)S(1)}, u32[]{:S(2)}, u32[]{:S(2)}) collective-permute-start(bf16[512,8,832]{0,2,1:T(8,128)(2,1)S(1)} %get-tuple-element.68), channel_id=1, source_target_pairs={{0,24},{8,0},{16,8},{24,16},{1,25},{9,1},{17,9},{25,17},{2,26},{10... | collective-permute-start | bytes 20447240 | tf_op jit(solution)/shard_map/ppermute | solution.py:87
  485.4 293.3 %collective-permute-start.7 = (bf16[512,8,832]{0,2,1:T(8,128)(2,1)S(1)}, bf16[512,8,832]{0,2,1:T(8,128)(2,1)S(1)}, u32[]{:S(2)}, u32[]{:S(2)}) collective-permute-start(bf16[512,8,832]{0,2,1:T(8,128)(2,1)S(1)} %get-tuple-element.69), channel_id=1, source_target_pairs={{0,16},{8,24},{16,0},{24,8},{1,17},{9,25},{17,1},{25,9},{2,18},{10... | collective-permute-start | bytes 20447240 | tf_op jit(solution)/shard_map/ppermute | solution.py:87
  486.3 292.4 %collective-permute-start.6 = (bf16[512,8,832]{0,2,1:T(8,128)(2,1)S(1)}, bf16[512,8,832]{0,2,1:T(8,128)(2,1)S(1)}, u32[]{:S(2)}, u32[]{:S(2)}) collective-permute-start(bf16[512,8,832]{0,2,1:T(8,128)(2,1)S(1)} %get-tuple-element.70), channel_id=1, source_target_pairs={{0,8},{8,16},{16,24},{24,0},{1,9},{9,17},{17,25},{25,1},{2,10},{10... | collective-permute-start | bytes 20447240 | tf_op jit(solution)/shard_map/ppermute | solution.py:87
  634.2 144.5 %copy-start.2 = (bf16[512,8,832]{0,2,1:T(8,128)(2,1)}, bf16[512,8,832]{0,2,1:T(8,128)(2,1)S(1)}, u32[]{:S(2)}) copy-start(bf16[512,8,832]{0,2,1:T(8,128)(2,1)S(1)} %collective-permute-done.8) | copy-start | bytes 20447236
  778.7 2.8 copy-start.4
  778.7 4.8 copy-start.6
  817.4 251.5 %all-gather.4.cloned.1.call-start = ((), (), s32[]{:S(2)}) async-start(), calls=%async_computation.8 | async-start | bytes 7667712 | tf_op jit(solution)/shard_map/all_gather | solution.py:104
  896.7 1.6 collective-permute-start.9
  898.3 8.4 collective-permute-start.10
  906.8 14.1 collective-permute-start.11
  920.9 8.3 collective-permute-start.12
  929.2 7.4 collective-permute-start.13
  1001.6 224.0 %reduce-scatter.11.cloned.1.call-start = ((), (), s32[]{:S(2)}) async-start(), calls=%async_computation.9 | async-start | bytes 7667712 | tf_op jit(solution)/shard_map/reduce_scatter | solution.py:98
  1068.9 13.6 copy-start.8
  1095.1 14.8 collective-permute-start.16
  1097.6 25.0 %collective-permute-start.15 = (f32[512,256]{1,0:T(8,128)S(1)}, f32[512,256]{1,0:T(8,128)S(1)}, u32[]{:S(2)}, u32[]{:S(2)}) collective-permute-start(f32[512,256]{1,0:T(8,128)S(1)} %get-tuple-element.79), channel_id=1, source_target_pairs={{0,16},{8,24},{16,0},{24,8},{1,17},{9,25},{17,1},{25,9},{2,18},{10... | collective-permute-start | bytes 1572872 | tf_op jit(solution)/shard_map/ppermute | solution.py:52
  1098.1 24.5 %collective-permute-start.14 = (f32[512,256]{1,0:T(8,128)S(1)}, f32[512,256]{1,0:T(8,128)S(1)}, u32[]{:S(2)}, u32[]{:S(2)}) collective-permute-start(f32[512,256]{1,0:T(8,128)S(1)} %get-tuple-element.77), channel_id=1, source_target_pairs={{0,8},{8,16},{16,24},{24,0},{1,9},{9,17},{17,25},{25,1},{2,10},{10... | collective-permute-start | bytes 1572872 | tf_op jit(solution)/shard_map/ppermute | solution.py:52
  1122.7 9.2 collective-permute-start.19
  1123.4 12.9 collective-permute-start.18
  1124.6 11.7 collective-permute-start.17
  1153.4 147.6 %reduce-scatter.13.cloned.1.call-start = ((), (), s32[]{:S(2)}) async-start(), calls=%async_computation.10 | async-start | bytes 7667712 | tf_op jit(solution)/shard_map/reduce_scatter | solution.py:98
  1171.0 306.6 %all-gather.6.cloned.1.call-start = ((), (), s32[]{:S(2)}) async-start(), calls=%async_computation.11 | async-start | bytes 7667712 | tf_op jit(solution)/shard_map/all_gather | solution.py:104
  1305.0 1.6 collective-permute-start.20
  1306.7 8.4 collective-permute-start.21
  1315.1 14.1 collective-permute-start.22
  1329.2 8.3 collective-permute-start.23
  1337.6 7.4 collective-permute-start.24
  1410.3 224.0 %reduce-scatter.15.cloned.1.call-start = ((), (), s32[]{:S(2)}) async-start(), calls=%async_computation.12 | async-start | bytes 7667712 | tf_op jit(solution)/shard_map/reduce_scatter | solution.py:98
  1477.6 13.6 copy-start.9
  1503.8 14.8 collective-permute-start.27
  1506.2 25.0 %collective-permute-start.26 = (f32[512,256]{1,0:T(8,128)S(1)}, f32[512,256]{1,0:T(8,128)S(1)}, u32[]{:S(2)}, u32[]{:S(2)}) collective-permute-start(f32[512,256]{1,0:T(8,128)S(1)} %get-tuple-element.76), channel_id=1, source_target_pairs={{0,16},{8,24},{16,0},{24,8},{1,17},{9,25},{17,1},{25,9},{2,18},{10... | collective-permute-start | bytes 1572872 | tf_op jit(solution)/shard_map/ppermute | solution.py:52
  1506.8 24.5 %collective-permute-start.25 = (f32[512,256]{1,0:T(8,128)S(1)}, f32[512,256]{1,0:T(8,128)S(1)}, u32[]{:S(2)}, u32[]{:S(2)}) collective-permute-start(f32[512,256]{1,0:T(8,128)S(1)} %get-tuple-element.74), channel_id=1, source_target_pairs={{0,8},{8,16},{16,24},{24,0},{1,9},{9,17},{17,25},{25,1},{2,10},{10... | collective-permute-start | bytes 1572872 | tf_op jit(solution)/shard_map/ppermute | solution.py:52
  1531.4 9.2 collective-permute-start.30
  1532.0 12.9 collective-permute-start.29
  1533.2 11.7 collective-permute-start.28
  1562.0 147.8 %reduce-scatter.17.cloned.1.call-start = ((), (), s32[]{:S(2)}) async-start(), calls=%async_computation.13 | async-start | bytes 7667712 | tf_op jit(solution)/shard_map/reduce_scatter | solution.py:98
  1579.6 306.8 %all-gather.8.cloned.1.call-start = ((), (), s32[]{:S(2)}) async-start(), calls=%async_computation.14 | async-start | bytes 7667712 | tf_op jit(solution)/shard_map/all_gather | solution.py:104
  1713.9 1.6 collective-permute-start.31
  1715.5 8.4 collective-permute-start.32
  1723.9 14.1 collective-permute-start.33
  1738.1 8.3 collective-permute-start.34
  1746.4 7.4 collective-permute-start.35
  1821.1 95.7 %collective-permute-start.41 = (f32[1664,256]{0,1:T(8,128)}, f32[1664,256]{0,1:T(8,128)}, u32[]{:S(2)}, u32[]{:S(2)}) collective-permute-start(f32[1664,256]{0,1:T(8,128)} %get-tuple-element.81), channel_id=1, source_target_pairs={{0,24},{8,0},{16,8},{24,16},{1,25},{9,1},{17,9},{25,17},{2,26},{10... | collective-permute-start | bytes 5111816 | tf_op jit(solution)/shard_map/ppermute | solution.py:30
  1823.5 93.9 %collective-permute-start.40 = (f32[1664,256]{0,1:T(8,128)}, f32[1664,256]{0,1:T(8,128)}, u32[]{:S(2)}, u32[]{:S(2)}) collective-permute-start(f32[1664,256]{0,1:T(8,128)} %get-tuple-element.81), channel_id=1, source_target_pairs={{0,16},{8,24},{16,0},{24,8},{1,17},{9,25},{17,1},{25,9},{2,18},{10... | collective-permute-start | bytes 5111816 | tf_op jit(solution)/shard_map/ppermute | solution.py:30
  1824.1 93.3 %collective-permute-start.39 = (f32[1664,256]{0,1:T(8,128)}, f32[1664,256]{0,1:T(8,128)}, u32[]{:S(2)}, u32[]{:S(2)}) collective-permute-start(f32[1664,256]{0,1:T(8,128)} %get-tuple-element.81), channel_id=1, source_target_pairs={{0,8},{8,16},{16,24},{24,0},{1,9},{9,17},{17,25},{25,1},{2,10},{10... | collective-permute-start | bytes 5111816 | tf_op jit(solution)/shard_map/ppermute | solution.py:30
  1886.5 13.6 copy-start.7
  1900.1 17.3 copy-start
  1913.9 28.7 %collective-permute-start.38 = (f32[512,256]{1,0:T(8,128)}, f32[512,256]{1,0:T(8,128)S(1)}, u32[]{:S(2)}, u32[]{:S(2)}) collective-permute-start(f32[512,256]{1,0:T(8,128)} %get-tuple-element.72), channel_id=1, source_target_pairs={{0,24},{8,0},{16,8},{24,16},{1,25},{9,1},{17,9},{25,17},{2,26},{10... | collective-permute-start | bytes 1572872 | tf_op jit(solution)/shard_map/ppermute | solution.py:52
  1916.3 26.3 %collective-permute-start.37 = (f32[512,256]{1,0:T(8,128)}, f32[512,256]{1,0:T(8,128)S(1)}, u32[]{:S(2)}, u32[]{:S(2)}) collective-permute-start(f32[512,256]{1,0:T(8,128)} %get-tuple-element.73), channel_id=1, source_target_pairs={{0,16},{8,24},{16,0},{24,8},{1,17},{9,25},{17,1},{25,9},{2,18},{10... | collective-permute-start | bytes 1572872 | tf_op jit(solution)/shard_map/ppermute | solution.py:52
  1916.8 25.7 %collective-permute-start.36 = (f32[512,256]{1,0:T(8,128)}, f32[512,256]{1,0:T(8,128)}, u32[]{:S(2)}, u32[]{:S(2)}) collective-permute-start(f32[512,256]{1,0:T(8,128)} %get-tuple-element.71), channel_id=1, source_target_pairs={{0,8},{8,16},{16,24},{24,0},{1,9},{9,17},{17,25},{25,1},{2,10},{10... | collective-permute-start | bytes 1572872 | tf_op jit(solution)/shard_map/ppermute | solution.py:52
Sparse Core Ops, SparseCore 0:
  471.7 74.3 reduce-scatter.6
  817.6 75.0 reduce-scatter.8
  1001.7 67.1 all-gather.3
  1153.5 72.1 reduce-scatter.10
  1227.8 73.1 reduce-scatter.12
  1410.4 67.1 all-gather.5
  1562.1 72.1 reduce-scatter.14
  1636.6 73.1 reduce-scatter.16
  1819.3 67.1 all-gather.7

commit v7 on v6

--- a/solution.py
+++ b/solution.py
@@ -63,8 +63,14 @@
     )
     gram = all_sum(partial_gram, ("col", "grad"))
     lower_factor = jnp.linalg.cholesky(gram)
-    return lax.linalg.triangular_solve(
-        lower_factor, rows, left_side=False, lower=True, transpose_a=True
+    identity = jnp.eye(gram.shape[0], dtype=gram.dtype)
+    inverse = lax.linalg.triangular_solve(lower_factor, identity, left_side=True, lower=True)
+    return lax.dot_general(
+        rows,
+        inverse,
+        (((1,), (1,)), ((), ())),
+        precision=lax.Precision.HIGHEST,
+        preferred_element_type=jnp.float32,
     )
 
 

time: 1960 us -> 1960 us (level)
  transfers between devices with their start and end apart: 51 -> 51, of which waited for: 37 -> 38; matrix products, arithmetic and copies ran while one was open for 7% -> 7% of each run, Pallas kernels for 0% -> 0%
where the time goes in v7:
time: 1960 us; the launch traced here: 1950 us
  waiting for transfers between devices  1310 us (67%)
  other arithmetic  216 us (11%)
  matrix products  199 us (10%)
  local copies, waits for them, and re-layouts  164 us (8%)
  starting transfers between devices  43.6 us (2%)
    ppermute x6, waiting for transfers between devices, shards(): lax.ppermute(outgoing, 'grad', [(i, (i + s) % n_grad) for i in range(n_gr...  583 us
    reduce_scatter x6, waiting for transfers between devices, sketch_of(): lax.psum_scatter(partial, 'col', scatter_dimension=0, tiled=True)  331 us
    all_gather x3, waiting for transfers between devices, shards(): lax.all_gather(basis_rows.astype(jnp.bfloat16).reshape(HALVES, half, -1),...  198 us
    ppermute x15, waiting for transfers between devices, all_sum(): lax.ppermute(value, axis, [(i, i ^ step) for i in range(size)])  108 us
    another operation x20, other arithmetic, orthonormal(): lower_factor = jnp.linalg.cholesky(gram)  104 us
    dot_general x6, matrix products, sketch_of(): lax.dot_general(chunk, rows, (((0,), (0,)), ((), ())), preferred_element_...  99.8 us
    optimization_barrier x1, local copies, waits for them, and re-layouts, shards(): lax.optimization_barrier((shift_gather(test_matrix), gradient))  64.7 us
    another operation x7, other arithmetic, orthonormal(): lax.linalg.triangular_solve(lower_factor, identity, left_side=True, lower...  59.1 us
  transfers between devices with their start and end apart: 51, of which 38 were waited for; matrix products, arithmetic and copies ran while one was open for 7% of the time, Pallas kernels for 0%

profile of v7, /device:TPU:0, one launch (start us, length us, event | category | flops | bytes accessed | tf_op | source)
XLA Modules:
  0.0 1948.4 jit_solution(4097757958011302660)
XLA Ops:
  12.3 5.9 collective-permute-done.2
  18.2 6.6 collective-permute-done.1
  25.8 64.7 %copy.13 = bf16[512,53248]{0,1:T(8,128)(2,1)} copy(bf16[512,53248]{1,0:T(8,128)(2,1)} %param.5) | data formatting | bytes 109051904 | tf_op jit(solution)/shard_map/optimization_barrier | solution.py:83
  90.5 35.6 %fusion.68 = (bf16[512,8,4,1,832]{0,4,3,2,1:T(8,128)(2,1)}, bf16[512,8,4,1,832]{0,4,3,2,1:T(8,128)(2,1)}) fusion(bf16[512,8,4,2,832]{0,4,3,2,1:T(8,128)(2,1)} %bitcast.170), kind=kLoop, calls=%fused_computation.152 | loop fusion | bytes 109051904 | tf_op jit(solution)/shard_map/slice | solution.py:88
  126.1 12.3 constant_dynamic-slice_fusion.4
  141.0 147.1 %collective-permute-done.5 = bf16[512,8,832]{0,2,1:T(8,128)(2,1)S(1)} collective-permute-done((bf16[512,8,832]{0,2,1:T(8,128)(2,1)S(1)}, bf16[512,8,832]{0,2,1:T(8,128)(2,1)S(1)}, u32[]{:S(2)}, u32[]{:S(2)}) %collective-permute-start.5) | collective-permute-done | bytes 6815776 | tf_op jit(solution)/shard_map/ppermute | solution.py:93
  288.1 144.7 %collective-permute-done.4 = bf16[512,8,832]{0,2,1:T(8,128)(2,1)S(1)} collective-permute-done((bf16[512,8,832]{0,2,1:T(8,128)(2,1)S(1)}, bf16[512,8,832]{0,2,1:T(8,128)(2,1)S(1)}, u32[]{:S(2)}, u32[]{:S(2)}) %collective-permute-start.4) | collective-permute-done | bytes 6815776 | tf_op jit(solution)/shard_map/ppermute | solution.py:93
  437.7 18.6 pad_maximum_fusion
  456.3 15.3 fusion.74
  471.6 12.9 constant_dynamic-slice_fusion.3
  487.2 147.0 %collective-permute-done.8 = bf16[512,8,832]{0,2,1:T(8,128)(2,1)S(1)} collective-permute-done((bf16[512,8,832]{0,2,1:T(8,128)(2,1)S(1)}, bf16[512,8,832]{0,2,1:T(8,128)(2,1)S(1)}, u32[]{:S(2)}, u32[]{:S(2)}) %collective-permute-start.8) | collective-permute-done | bytes 6815776 | tf_op jit(solution)/shard_map/ppermute | solution.py:93
  634.2 144.5 %collective-permute-done.7 = bf16[512,8,832]{0,2,1:T(8,128)(2,1)S(1)} collective-permute-done((bf16[512,8,832]{0,2,1:T(8,128)(2,1)S(1)}, bf16[512,8,832]{0,2,1:T(8,128)(2,1)S(1)}, u32[]{:S(2)}, u32[]{:S(2)}) %collective-permute-start.7) | collective-permute-done | bytes 6815776 | tf_op jit(solution)/shard_map/ppermute | solution.py:93
  783.5 18.6 pad_maximum_fusion.1
  802.1 15.4 fusion.75
  818.9 73.7 %reduce-scatter.9.cloned.1.call-done = f32[832,256]{1,0:T(8,128)} async-done(((f32[6656,256]{1,0:T(8,128)}), f32[832,256]{1,0:T(8,128)}) %reduce-scatter.9.cloned.1.call-update) | async-done | bytes 851984 | tf_op jit(solution)/shard_map/reduce_scatter | solution.py:104
  898.4 8.3 collective-permute-done.10
  907.4 13.4 collective-permute-done.11
  922.4 6.8 collective-permute-done.12
  936.9 11.7 cholesky.172
  948.7 9.8 custom-call.15
  959.0 12.1 cholesky.189
  977.1 19.7 %custom-call.16 = f32[2,128,128]{1,2,0:T(8,128)S(1)} custom-call(f32[2,128,128]{2,1,0:T(8,128)S(1)} %get-tuple-element.28), custom_call_target="InvertDiagBlocksLowerTriangular" | custom-call | tf_op jit(solution)/shard_map/triangular_solve/custom-call.0 | solution.py:67
  1000.4 67.1 %all-gather.4.cloned.1.call-done = bf16[2,6656,256]{2,1,0:T(8,128)(2,1)} async-done(((bf16[2,832,256]{2,1,0:T(8,128)(2,1)}), bf16[2,6656,256]{2,1,0:T(8,128)(2,1)}) %all-gather.4.cloned.1.call-update) | async-done | bytes 6815760 | tf_op jit(solution)/shard_map/all_gather | solution.py:110
  1067.5 13.6 fusion.5
  1081.1 12.5 fusion.7
  1097.2 11.3 collective-permute-done.16
  1108.5 12.6 collective-permute-done.15
  1124.1 6.4 collective-permute-done.19
  1134.8 17.0 fusion.35
  1151.9 17.6 fusion.34
  1170.0 54.2 %reduce-scatter.11.cloned.1.call-done = f32[832,256]{1,0:T(8,128)} async-done(((f32[6656,256]{1,0:T(8,128)}), f32[832,256]{1,0:T(8,128)}) %reduce-scatter.11.cloned.1.call-update) | async-done | bytes 851984 | tf_op jit(solution)/shard_map/reduce_scatter | solution.py:104
  1225.4 74.1 %reduce-scatter.13.cloned.1.call-done = f32[832,256]{1,0:T(8,128)} async-done(((f32[6656,256]{1,0:T(8,128)}), f32[832,256]{1,0:T(8,128)}) %reduce-scatter.13.cloned.1.call-update) | async-done | bytes 851984 | tf_op jit(solution)/shard_map/reduce_scatter | solution.py:104
  1305.3 8.3 collective-permute-done.21
  1314.3 13.4 collective-permute-done.22
  1329.3 6.8 collective-permute-done.23
  1337.6 5.9 collective-permute-done.24
  1343.8 11.7 cholesky.206
  1355.5 9.8 custom-call.17
  1365.8 11.9 cholesky.223
  1384.3 19.7 %custom-call.18 = f32[2,128,128]{1,2,0:T(8,128)S(1)} custom-call(f32[2,128,128]{2,1,0:T(8,128)S(1)} %get-tuple-element.29), custom_call_target="InvertDiagBlocksLowerTriangular" | custom-call | tf_op jit(solution)/shard_map/triangular_solve/custom-call.0 | solution.py:67
  1407.6 67.1 %all-gather.6.cloned.1.call-done = bf16[2,6656,256]{2,1,0:T(8,128)(2,1)} async-done(((bf16[2,832,256]{2,1,0:T(8,128)(2,1)}), bf16[2,6656,256]{2,1,0:T(8,128)(2,1)}) %all-gather.6.cloned.1.call-update) | async-done | bytes 6815760 | tf_op jit(solution)/shard_map/all_gather | solution.py:110
  1474.7 13.6 fusion.3
  1488.3 12.5 fusion.8
  1504.4 11.3 collective-permute-done.27
  1515.7 12.6 collective-permute-done.26
  1531.5 6.2 collective-permute-done.30
  1542.0 17.0 fusion.33
  1559.1 17.6 fusion.32
  1576.9 54.4 %reduce-scatter.15.cloned.1.call-done = f32[832,256]{1,0:T(8,128)} async-done(((f32[6656,256]{1,0:T(8,128)}), f32[832,256]{1,0:T(8,128)}) %reduce-scatter.15.cloned.1.call-update) | async-done | bytes 851984 | tf_op jit(solution)/shard_map/reduce_scatter | solution.py:104
  1632.6 74.3 %reduce-scatter.17.cloned.1.call-done = f32[832,256]{1,0:T(8,128)} async-done(((f32[6656,256]{1,0:T(8,128)}), f32[832,256]{1,0:T(8,128)}) %reduce-scatter.17.cloned.1.call-update) | async-done | bytes 851984 | tf_op jit(solution)/shard_map/reduce_scatter | solution.py:104
  1712.6 8.3 collective-permute-done.32
  1721.7 13.4 collective-permute-done.33
  1736.6 6.8 collective-permute-done.34
  1745.0 5.9 collective-permute-done.35
  1751.1 11.7 cholesky.240
  1762.9 9.8 custom-call.19
  1773.2 11.9 cholesky.257
  1791.7 19.7 %custom-call.20 = f32[2,128,128]{1,2,0:T(8,128)S(1)} custom-call(f32[2,128,128]{2,1,0:T(8,128)S(1)} %get-tuple-element.30), custom_call_target="InvertDiagBlocksLowerTriangular" | custom-call | tf_op jit(solution)/shard_map/triangular_solve/custom-call.0 | solution.py:67
  1819.1 63.5 %all-gather.8.cloned.1.call-done = bf16[2,6656,256]{2,1,0:T(8,128)(2,1)} async-done(((bf16[2,832,256]{2,1,0:T(8,128)(2,1)}), bf16[2,6656,256]{2,1,0:T(8,128)(2,1)}) %all-gather.8.cloned.1.call-update) | async-done | bytes 6815760 | tf_op jit(solution)/shard_map/all_gather | solution.py:110
  1882.6 13.6 fusion.1
  1896.2 12.5 fusion.9
  1919.4 6.2 rev.3
  1925.6 6.7 fusion
  1932.3 6.7 collective-permute-done.37
  (202 shorter events, 139.7 us)
Async XLA Ops:
  7.2 810.6 %reduce-scatter.7.cloned.1.call-start = ((), (), s32[]{:S(2)}) async-start(), calls=%async_computation.6 | async-start | bytes 7667712 | tf_op jit(solution)/shard_map/reduce_scatter | solution.py:104
  7.2 11.0 collective-permute-start.2
  11.2 13.6 collective-permute-start.1
  11.7 13.1 collective-permute-start
  138.5 149.6 %collective-permute-start.5 = (bf16[512,8,832]{0,2,1:T(8,128)(2,1)S(1)}, bf16[512,8,832]{0,2,1:T(8,128)(2,1)S(1)}, u32[]{:S(2)}, u32[]{:S(2)}) collective-permute-start(bf16[512,8,832]{0,2,1:T(8,128)(2,1)S(1)} %get-tuple-element.64), channel_id=1, source_target_pairs={{0,24},{8,0},{16,8},{24,16},{1,25},{9,1},{17,9},{25,17},{2,26},{10... | collective-permute-start | bytes 20447240 | tf_op jit(solution)/shard_map/ppermute | solution.py:93
  139.0 293.8 %collective-permute-start.4 = (bf16[512,8,832]{0,2,1:T(8,128)(2,1)S(1)}, bf16[512,8,832]{0,2,1:T(8,128)(2,1)S(1)}, u32[]{:S(2)}, u32[]{:S(2)}) collective-permute-start(bf16[512,8,832]{0,2,1:T(8,128)(2,1)S(1)} %get-tuple-element.65), channel_id=1, source_target_pairs={{0,16},{8,24},{16,0},{24,8},{1,17},{9,25},{17,1},{25,9},{2,18},{10... | collective-permute-start | bytes 20447240 | tf_op jit(solution)/shard_map/ppermute | solution.py:93
  140.2 292.6 %collective-permute-start.3 = (bf16[512,8,832]{0,2,1:T(8,128)(2,1)S(1)}, bf16[512,8,832]{0,2,1:T(8,128)(2,1)S(1)}, u32[]{:S(2)}, u32[]{:S(2)}) collective-permute-start(bf16[512,8,832]{0,2,1:T(8,128)(2,1)S(1)} %get-tuple-element.66), channel_id=1, source_target_pairs={{0,8},{8,16},{16,24},{24,0},{1,9},{9,17},{17,25},{25,1},{2,10},{10... | collective-permute-start | bytes 20447240 | tf_op jit(solution)/shard_map/ppermute | solution.py:93
  288.1 144.7 %copy-start = (bf16[512,8,832]{0,2,1:T(8,128)(2,1)}, bf16[512,8,832]{0,2,1:T(8,128)(2,1)S(1)}, u32[]{:S(2)}) copy-start(bf16[512,8,832]{0,2,1:T(8,128)(2,1)S(1)} %collective-permute-done.5) | copy-start | bytes 20447236
  432.8 2.7 copy-start.2
  432.8 4.9 copy-start.4
  471.6 421.0 %reduce-scatter.9.cloned.1.call-start = ((), (), s32[]{:S(2)}) async-start(), calls=%async_computation.7 | async-start | bytes 7667712 | tf_op jit(solution)/shard_map/reduce_scatter | solution.py:104
  484.6 149.6 %collective-permute-start.8 = (bf16[512,8,832]{0,2,1:T(8,128)(2,1)S(1)}, bf16[512,8,832]{0,2,1:T(8,128)(2,1)S(1)}, u32[]{:S(2)}, u32[]{:S(2)}) collective-permute-start(bf16[512,8,832]{0,2,1:T(8,128)(2,1)S(1)} %get-tuple-element.68), channel_id=1, source_target_pairs={{0,24},{8,0},{16,8},{24,16},{1,25},{9,1},{17,9},{25,17},{2,26},{10... | collective-permute-start | bytes 20447240 | tf_op jit(solution)/shard_map/ppermute | solution.py:93
  485.4 293.3 %collective-permute-start.7 = (bf16[512,8,832]{0,2,1:T(8,128)(2,1)S(1)}, bf16[512,8,832]{0,2,1:T(8,128)(2,1)S(1)}, u32[]{:S(2)}, u32[]{:S(2)}) collective-permute-start(bf16[512,8,832]{0,2,1:T(8,128)(2,1)S(1)} %get-tuple-element.69), channel_id=1, source_target_pairs={{0,16},{8,24},{16,0},{24,8},{1,17},{9,25},{17,1},{25,9},{2,18},{10... | collective-permute-start | bytes 20447240 | tf_op jit(solution)/shard_map/ppermute | solution.py:93
  486.3 292.4 %collective-permute-start.6 = (bf16[512,8,832]{0,2,1:T(8,128)(2,1)S(1)}, bf16[512,8,832]{0,2,1:T(8,128)(2,1)S(1)}, u32[]{:S(2)}, u32[]{:S(2)}) collective-permute-start(bf16[512,8,832]{0,2,1:T(8,128)(2,1)S(1)} %get-tuple-element.70), channel_id=1, source_target_pairs={{0,8},{8,16},{16,24},{24,0},{1,9},{9,17},{17,25},{25,1},{2,10},{10... | collective-permute-start | bytes 20447240 | tf_op jit(solution)/shard_map/ppermute | solution.py:93
  634.2 144.5 %copy-start.1 = (bf16[512,8,832]{0,2,1:T(8,128)(2,1)}, bf16[512,8,832]{0,2,1:T(8,128)(2,1)S(1)}, u32[]{:S(2)}) copy-start(bf16[512,8,832]{0,2,1:T(8,128)(2,1)S(1)} %collective-permute-done.8) | copy-start | bytes 20447236
  778.7 2.8 copy-start.3
  778.7 4.8 copy-start.5
  817.4 250.0 %all-gather.4.cloned.1.call-start = ((), (), s32[]{:S(2)}) async-start(), calls=%async_computation.8 | async-start | bytes 7667712 | tf_op jit(solution)/shard_map/all_gather | solution.py:110
  896.7 1.6 collective-permute-start.9
  898.3 8.4 collective-permute-start.10
  906.8 14.1 collective-permute-start.11
  920.9 8.3 collective-permute-start.12
  929.2 7.4 collective-permute-start.13
  1000.2 224.0 %reduce-scatter.11.cloned.1.call-start = ((), (), s32[]{:S(2)}) async-start(), calls=%async_computation.9 | async-start | bytes 7667712 | tf_op jit(solution)/shard_map/reduce_scatter | solution.py:104
  1067.5 13.6 copy-start.8
  1093.7 14.8 collective-permute-start.16
  1096.1 25.0 %collective-permute-start.15 = (f32[512,256]{1,0:T(8,128)S(1)}, f32[512,256]{1,0:T(8,128)S(1)}, u32[]{:S(2)}, u32[]{:S(2)}) collective-permute-start(f32[512,256]{1,0:T(8,128)S(1)} %get-tuple-element.79), channel_id=1, source_target_pairs={{0,16},{8,24},{16,0},{24,8},{1,17},{9,25},{17,1},{25,9},{2,18},{10... | collective-permute-start | bytes 1572872 | tf_op jit(solution)/shard_map/ppermute | solution.py:52
  1096.7 24.5 %collective-permute-start.14 = (f32[512,256]{1,0:T(8,128)S(1)}, f32[512,256]{1,0:T(8,128)S(1)}, u32[]{:S(2)}, u32[]{:S(2)}) collective-permute-start(f32[512,256]{1,0:T(8,128)S(1)} %get-tuple-element.77), channel_id=1, source_target_pairs={{0,8},{8,16},{16,24},{24,0},{1,9},{9,17},{17,25},{25,1},{2,10},{10... | collective-permute-start | bytes 1572872 | tf_op jit(solution)/shard_map/ppermute | solution.py:52
  1121.3 9.2 collective-permute-start.19
  1121.9 12.9 collective-permute-start.18
  1123.1 11.7 collective-permute-start.17
  1151.9 147.6 %reduce-scatter.13.cloned.1.call-start = ((), (), s32[]{:S(2)}) async-start(), calls=%async_computation.10 | async-start | bytes 7667712 | tf_op jit(solution)/shard_map/reduce_scatter | solution.py:104
  1169.5 305.1 %all-gather.6.cloned.1.call-start = ((), (), s32[]{:S(2)}) async-start(), calls=%async_computation.11 | async-start | bytes 7667712 | tf_op jit(solution)/shard_map/all_gather | solution.py:110
  1303.6 1.6 collective-permute-start.20
  1305.2 8.4 collective-permute-start.21
  1313.7 14.1 collective-permute-start.22
  1327.8 8.3 collective-permute-start.23
  1336.1 7.4 collective-permute-start.24
  1407.3 224.0 %reduce-scatter.15.cloned.1.call-start = ((), (), s32[]{:S(2)}) async-start(), calls=%async_computation.12 | async-start | bytes 7667712 | tf_op jit(solution)/shard_map/reduce_scatter | solution.py:104
  1474.7 13.6 copy-start.9
  1500.9 14.8 collective-permute-start.27
  1503.3 25.0 %collective-permute-start.26 = (f32[512,256]{1,0:T(8,128)S(1)}, f32[512,256]{1,0:T(8,128)S(1)}, u32[]{:S(2)}, u32[]{:S(2)}) collective-permute-start(f32[512,256]{1,0:T(8,128)S(1)} %get-tuple-element.76), channel_id=1, source_target_pairs={{0,16},{8,24},{16,0},{24,8},{1,17},{9,25},{17,1},{25,9},{2,18},{10... | collective-permute-start | bytes 1572872 | tf_op jit(solution)/shard_map/ppermute | solution.py:52
  1503.9 24.5 %collective-permute-start.25 = (f32[512,256]{1,0:T(8,128)S(1)}, f32[512,256]{1,0:T(8,128)S(1)}, u32[]{:S(2)}, u32[]{:S(2)}) collective-permute-start(f32[512,256]{1,0:T(8,128)S(1)} %get-tuple-element.74), channel_id=1, source_target_pairs={{0,8},{8,16},{16,24},{24,0},{1,9},{9,17},{17,25},{25,1},{2,10},{10... | collective-permute-start | bytes 1572872 | tf_op jit(solution)/shard_map/ppermute | solution.py:52
  1528.5 9.2 collective-permute-start.30
  1529.1 12.9 collective-permute-start.29
  1530.3 11.7 collective-permute-start.28
  1559.1 147.7 %reduce-scatter.17.cloned.1.call-start = ((), (), s32[]{:S(2)}) async-start(), calls=%async_computation.13 | async-start | bytes 7667712 | tf_op jit(solution)/shard_map/reduce_scatter | solution.py:104
  1576.7 305.9 %all-gather.8.cloned.1.call-start = ((), (), s32[]{:S(2)}) async-start(), calls=%async_computation.14 | async-start | bytes 7667712 | tf_op jit(solution)/shard_map/all_gather | solution.py:110
  1710.9 1.6 collective-permute-start.31
  1712.6 8.4 collective-permute-start.32
  1721.0 14.1 collective-permute-start.33
  1735.1 8.3 collective-permute-start.34
  1743.4 7.4 collective-permute-start.35
  1815.3 98.9 %collective-permute-start.41 = (f32[1664,256]{1,0:T(8,128)}, f32[1664,256]{1,0:T(8,128)S(1)}, u32[]{:S(2)}, u32[]{:S(2)}) collective-permute-start(f32[1664,256]{1,0:T(8,128)} %get-tuple-element.81), channel_id=1, source_target_pairs={{0,24},{8,0},{16,8},{24,16},{1,25},{9,1},{17,9},{25,17},{2,26},{10... | collective-permute-start | bytes 5111816 | tf_op jit(solution)/shard_map/ppermute | solution.py:30
  1817.7 97.1 %collective-permute-start.40 = (f32[1664,256]{1,0:T(8,128)}, f32[1664,256]{1,0:T(8,128)}, u32[]{:S(2)}, u32[]{:S(2)}) collective-permute-start(f32[1664,256]{1,0:T(8,128)} %get-tuple-element.81), channel_id=1, source_target_pairs={{0,16},{8,24},{16,0},{24,8},{1,17},{9,25},{17,1},{25,9},{2,18},{10... | collective-permute-start | bytes 5111816 | tf_op jit(solution)/shard_map/ppermute | solution.py:30
  1818.3 96.5 %collective-permute-start.39 = (f32[1664,256]{1,0:T(8,128)}, f32[1664,256]{1,0:T(8,128)}, u32[]{:S(2)}, u32[]{:S(2)}) collective-permute-start(f32[1664,256]{1,0:T(8,128)} %get-tuple-element.81), channel_id=1, source_target_pairs={{0,8},{8,16},{16,24},{24,0},{1,9},{9,17},{17,25},{25,1},{2,10},{10... | collective-permute-start | bytes 5111816 | tf_op jit(solution)/shard_map/ppermute | solution.py:30
  1882.6 13.6 copy-start.7
  1908.7 1.4 copy-start.6
  1911.3 21.0 %collective-permute-start.38 = (f32[512,256]{1,0:T(8,128)}, f32[512,256]{1,0:T(8,128)}, u32[]{:S(2)}, u32[]{:S(2)}) collective-permute-start(f32[512,256]{1,0:T(8,128)} %get-tuple-element.72), channel_id=1, source_target_pairs={{0,24},{8,0},{16,8},{24,16},{1,25},{9,1},{17,9},{25,17},{2,26},{10... | collective-permute-start | bytes 1572872 | tf_op jit(solution)/shard_map/ppermute | solution.py:52
  1913.7 25.3 %collective-permute-start.37 = (f32[512,256]{1,0:T(8,128)}, f32[512,256]{1,0:T(8,128)}, u32[]{:S(2)}, u32[]{:S(2)}) collective-permute-start(f32[512,256]{1,0:T(8,128)} %get-tuple-element.73), channel_id=1, source_target_pairs={{0,16},{8,24},{16,0},{24,8},{1,17},{9,25},{17,1},{25,9},{2,18},{10... | collective-permute-start | bytes 1572872 | tf_op jit(solution)/shard_map/ppermute | solution.py:52
  1914.2 24.8 %collective-permute-start.36 = (f32[512,256]{1,0:T(8,128)}, f32[512,256]{1,0:T(8,128)}, u32[]{:S(2)}, u32[]{:S(2)}) collective-permute-start(f32[512,256]{1,0:T(8,128)} %get-tuple-element.71), channel_id=1, source_target_pairs={{0,8},{8,16},{16,24},{24,0},{1,9},{9,17},{17,25},{25,1},{2,10},{10... | collective-permute-start | bytes 1572872 | tf_op jit(solution)/shard_map/ppermute | solution.py:52
Sparse Core Ops, SparseCore 0:
  471.7 74.3 reduce-scatter.6
  817.6 75.0 reduce-scatter.8
  1000.3 67.1 all-gather.3
  1152.0 72.1 reduce-scatter.10
  1226.3 73.1 reduce-scatter.12
  1407.5 67.1 all-gather.5
  1559.2 72.1 reduce-scatter.14
  1633.7 73.1 reduce-scatter.16
  1815.4 67.1 all-gather.7
